TPU v7x, 128 devices: a whole 4x4x4 slice. The times are simulated.
128 devices in a mesh: dp: 16 (over y, z_hi, core), mp: 8 (over x, z_lo).
Axes of the slice: x: 4, y: 4, z: 4 (z_hi: 2, z_lo: 2; z = z_hi * 2 + z_lo), core: 2. Of those that a mesh axis runs over, the one named last changes fastest.
Arguments:
- features: bfloat16 [8192, 8192], P('mp', 'dp'), may hold values from -6 to 6
- cotangent: bfloat16 [8192, 8192], P('mp', 'dp'), may hold values from -6 to 6
- block_perm: int32 [16, 512], P('mp'), may hold values from 0 to 511, each once within a row
- w_gate: bfloat16 [16, 512, 2048], P('mp'), may hold values from -0.25 to 0.25
- w_up: bfloat16 [16, 512, 2048], P('mp'), may hold values from -0.25 to 0.25
- w_down: bfloat16 [16, 2048, 512], P('mp'), may hold values from -0.125 to 0.125
Outputs:
- outputs: bfloat16 [8192, 8192], P('mp', 'dp')
- d_features: bfloat16 [8192, 8192], P('mp', 'dp')
- gate_grad: float32 [16, 512, 2048], P('mp', 'dp')
- up_grad: float32 [16, 512, 2048], P('mp', 'dp')
- down_grad: float32 [16, 2048, 512], P('mp', 'dp')
Inputs may be any that keep to these rules, and one draw needn't show every extreme that they name: Each row of block_perm names every number below 512 exactly once.
All inputs are finite; a program needn't handle non-finite values.
Results may differ from a plain program's by a relative error of at most 0.012.
Values may be sent and summed in bfloat16 or wider, within the bound.
No kernel may reach another device: no remote copies, remote signals or barrier semaphores. Data moves between devices by JAX's collectives and lax.ppermute only.
A program may use at most 128 MiB of HBM per device.

v0:
```python
import jax
import jax.numpy as jnp
from jax import lax
from jax.sharding import Mesh
from jax.sharding import PartitionSpec as P


input_scale = 2.0
output_scale = 0.5


def perm_matrix(block_perm):
    count = block_perm.shape[1]
    targets = lax.broadcasted_iota(jnp.int32, (1, 1, count), 2)
    return (block_perm[:, :, None] == targets).astype(jnp.bfloat16)


def own_bits():
    dy = lax.axis_index("dy")
    return (lax.axis_index("core"), dy % 2, lax.axis_index("dz"), dy // 2)


def relabel(x, axis):
    core, dy0, dz, dy1 = own_bits()
    for offset, bit in ((0, dy1), (1, dy0), (2, dz), (3, core)):
        x = jnp.where(bit == 1, jnp.flip(x, axis + offset), x)
    return x


def tree_reduce(acc, order, first, dims=("dy1", "dy0", "dz", "core")):
    n_dy = lax.axis_size("dy")
    swaps = {
        "core": ("core", [(0, 1), (1, 0)]),
        "dy0": ("dy", [(i, i ^ 1) for i in range(n_dy)]),
        "dz": ("dz", [(0, 1), (1, 0)]),
        "dy1": ("dy", [(i, i ^ 2) for i in range(n_dy)]),
    }
    dims = list(dims)
    total = None
    for bit in order:
        axis = first + dims.index(bit)
        dims.remove(bit)
        name, pairs = swaps[bit]
        got = lax.ppermute(lax.index_in_dim(acc, 1, axis, keepdims=False), name, perm=pairs)
        total = lax.index_in_dim(acc, 0, axis, keepdims=False).astype(
            jnp.float32
        ) + got.astype(jnp.float32)
        acc = total.astype(jnp.bfloat16)
    return total


ORDER_A = ("core", "dy0", "dz", "dy1")
ORDER_B = ("core", "dz", "dy0", "dy1")


def local(features, cotangent, block_perm, w_gate, w_up, w_down):
    tok_count = features.shape[1]
    blocks_here = w_gate.shape[0]
    inner = w_gate.shape[1]
    hidden_width = w_gate.shape[2]
    n_mp = lax.axis_size("mp")
    n_dp = lax.axis_size("dy") * lax.axis_size("dz") * lax.axis_size("core")
    block_total = blocks_here * n_mp
    piece = inner // block_total
    s_here = features.shape[0] // (block_total * piece)
    grad_scale = (tok_count * n_dp) ** (-0.5)

    both = jnp.stack([features, cotangent]).reshape(2, s_here, block_total, piece, tok_count)
    both = lax.all_to_all(both, "mp", split_axis=2, concat_axis=1, tiled=True)
    feat_blocks = both[0]
    cot_blocks = both[1]

    onehot = perm_matrix(block_perm)
    feat_rows = feat_blocks.transpose(1, 0, 2, 3).reshape(blocks_here, inner, tok_count)
    feat_p = jnp.einsum(
        "bij,bjt->bit", onehot, feat_rows, preferred_element_type=jnp.float32
    ).astype(jnp.bfloat16)

    gate = (
        jnp.einsum("bit,bih->bth", feat_p, w_gate, preferred_element_type=jnp.float32)
        * input_scale
    )
    up = (
        jnp.einsum("bit,bih->bth", feat_p, w_up, preferred_element_type=jnp.float32)
        * input_scale
    )
    sig = jax.nn.sigmoid(gate)
    act = gate * sig
    hidden = (act * up).astype(jnp.bfloat16)
    down_view = w_down.reshape(blocks_here, hidden_width, block_total, piece)

    n_dy = lax.axis_size("dy")
    cot_rows = cot_blocks.transpose(1, 0, 2, 3).reshape(blocks_here, inner, tok_count)
    n_chunk = 4 * n_dy
    dp_index = (lax.axis_index("dy") * 2 + lax.axis_index("dz")) * 2 + lax.axis_index("core")
    down_nat = (
        jnp.einsum("bth,bjt->bhj", hidden, cot_rows, preferred_element_type=jnp.float32)
        * (output_scale * grad_scale)
    ).astype(jnp.bfloat16)
    down_nat = down_nat.reshape(blocks_here, n_chunk, hidden_width // n_chunk, inner)
    down_part = jnp.stack(
        [lax.dynamic_index_in_dim(down_nat, c ^ dp_index, 1, keepdims=False) for c in range(n_chunk)],
        axis=1,
    ).reshape((blocks_here, n_dy // 2, 2, 2, 2) + down_nat.shape[2:])
    down_grad = jnp.stack(
        [tree_reduce(down_part[b], (ORDER_A, ORDER_B)[b % 2], 0) for b in range(blocks_here)]
    )

    mixed = (
        jnp.einsum("bth,bhsk->sbkt", hidden, down_view, preferred_element_type=jnp.float32)
        * output_scale
    ).astype(jnp.bfloat16)
    outputs = lax.all_to_all(mixed, "mp", split_axis=0, concat_axis=1, tiled=True).reshape(
        features.shape
    )

    d_hidden = (
        jnp.einsum("sbkt,bhsk->bth", cot_blocks, down_view, preferred_element_type=jnp.float32)
        * output_scale
    )
    d_gate = (d_hidden * up * (sig * (1.0 + gate * (1.0 - sig)))).astype(jnp.bfloat16)
    d_up = (d_hidden * act).astype(jnp.bfloat16)

    feat_l = relabel(
        feat_p.reshape(blocks_here, n_dy // 2, 2, 2, 2, inner // (4 * n_dy), tok_count), 1
    )
    d_both = jnp.stack([d_gate, d_up])
    gate_up_part = (
        jnp.einsum(
            "bwyzcrt,gbth->gbwyzcrh", feat_l, d_both, preferred_element_type=jnp.float32
        )
        * (input_scale * grad_scale)
    ).astype(jnp.bfloat16)
    gate_core = tree_reduce(gate_up_part[0], ORDER_A[:1], 1).astype(jnp.bfloat16)
    up_core = tree_reduce(gate_up_part[1], ORDER_B[:1], 1).astype(jnp.bfloat16)
    gate_core, up_core, d_gate, d_up = lax.optimization_barrier((gate_core, up_core, d_gate, d_up))
    rest = ("dy1", "dy0", "dz")
    gate_grad = tree_reduce(gate_core, ORDER_A[1:], 1, rest)
    up_grad = tree_reduce(up_core, ORDER_B[1:], 1, rest)

    d_mixed_p = (
        (
            jnp.einsum("bth,bih->bit", d_gate, w_gate, preferred_element_type=jnp.float32)
            + jnp.einsum("bth,bih->bit", d_up, w_up, preferred_element_type=jnp.float32)
        )
        * input_scale
    ).astype(jnp.bfloat16)
    d_mixed = jnp.einsum(
        "bij,bit->bjt", onehot, d_mixed_p, preferred_element_type=jnp.float32
    ).astype(jnp.bfloat16)
    d_mixed = d_mixed.reshape(blocks_here, block_total, piece, tok_count).transpose(1, 0, 2, 3)

    d_features = lax.all_to_all(d_mixed, "mp", split_axis=0, concat_axis=1, tiled=True).reshape(
        features.shape
    )
    return (outputs, d_features, gate_grad, up_grad, down_grad)


def solution(mesh):
    dp_size = mesh.shape["dp"]
    devices = mesh.devices.reshape(dp_size // 4, 2, 2, mesh.shape["mp"])
    mesh = Mesh(devices, ("dy", "dz", "core", "mp"))
    dp = ("dy", "dz", "core")
    placed = (
        P("mp", dp),
        P("mp", dp),
        P("mp", None),
        P("mp", None, None),
        P("mp", None, None),
        P("mp", None, None),
    )

    return jax.shard_map(
        local,
        mesh=mesh,
        in_specs=placed,
        out_specs=(
            P("mp", dp),
            P("mp", dp),
            P("mp", dp, None),
            P("mp", dp, None),
            P("mp", dp, None),
        ),
        check_vma=False,
    )
```

profile of v0, /device:TPU:0, one launch (start us, length us, event | category | flops | bytes accessed | tf_op | source)
XLA Modules:
  0.0 216.3 jit_solution(4125935554054765272)
XLA Ops:
  0.6 1.7 pad_maximum_fusion
  2.4 1.6 copy.101
  4.0 5.8 %all-to-all-start = ((bf16[2,2,16,32,512]{4,3,1,0,2:T(8,128)(2,1)}), bf16[2,2,16,32,512]{4,3,1,0,2:T(8,128)(2,1)S(1)}, u32[]{:S(2)}, u32[]{:S(2)}) async-start(bf16[2,2,16,32,512]{4,3,1,0,2:T(8,128)(2,1)} %copy.101), calls=%async_computation | async-start | bytes 4194304 | tf_op jit(solution)/shard_map/all_to_all | solution.py:69
  9.7 6.3 %copy.108 = bf16[2,2048,512]{1,2,0:T(8,128)(2,1)} copy(bf16[2,2048,512]{2,1,0:T(8,128)(2,1)} %param.11) | data formatting | bytes 8388608 | tf_op args[5]
  16.0 25.0 %all-to-all-done = bf16[2,2,16,32,512]{4,3,1,0,2:T(8,128)(2,1)S(1)} async-done(((bf16[2,2,16,32,512]{4,3,1,0,2:T(8,128)(2,1)}), bf16[2,2,16,32,512]{4,3,1,0,2:T(8,128)(2,1)S(1)}, u32[]{:S(2)}, u32[]{:S(2)}) %all-to-all-start) | async-done | bytes 2097184 | tf_op jit(solution)/shard_map/all_to_all | solution.py:69
  43.6 2.4 %fusion.33 = f32[2,512,2048]{2,1,0:T(8,128)S(1)} fusion(bf16[2,512,512]{2,1,0:T(8,128)(2,1)S(1)} %fusion.14, bf16[2,512,2048]{2,1,0:T(8,128)(2,1)S(1)} %copy-done.4), kind=kOutput, calls=%fused_computation.115 | convolution fusion | flops 2147483648 | bytes 13631488 | tf_op jit(solution)/shard_map/bit,bih->bth/dot_general | solution.py:84
  46.0 5.7 %fusion.32 = f32[2,512,2048]{2,1,0:T(8,128)} fusion(bf16[2,512,512]{2,1,0:T(8,128)(2,1)S(1)} %fusion.14, bf16[2,512,2048]{2,1,0:T(8,128)(2,1)S(1)} %copy-done.6), kind=kOutput, calls=%fused_computation.114 | convolution fusion | flops 2147483648 | bytes 13631488 | tf_op jit(solution)/shard_map/bit,bih->bth/dot_general | solution.py:80
  51.8 13.4 %multiply_convert_fusion.3 = (bf16[2,512,2048]{2,1,0:T(8,128)(2,1)}, bf16[2,512,2048]{2,1,0:T(8,128)(2,1)}, bf16[2,512,2048]{2,1,0:T(8,128)(2,1)}) fusion(f32[2,512,2048]{2,1,0:T(8,128)S(1)} %fusion.33, f32[2,512,2048]{2,1,0:T(8,128)} %fusion.32, bf16[16,2,32,512]{3,2,0,1:T(8,128)(2,1)S(1)} %bitcast.240, bf16[2,2048,16,32]{1,3,2,0:T(8,128)(2,1)} %bitcast.231), kind=kOutput, calls=%fused_computation.8 | convolution fusion | flops 2185232384 | bytes 34603008 | tf_op jit(solution)/shard_map/sbkt,bhsk->bth/dot_general | solution.py:118
  65.2 5.8 %fusion.34 = f32[2,512,512]{1,2,0:S(1)} fusion(bf16[2,512,2048]{2,1,0:T(8,128)(2,1)} %get-tuple-element.14, bf16[2,2048,512]{2,1,0:T(8,128)(2,1)} %param.11), kind=kOutput, calls=%fused_computation.116 | convolution fusion | flops 2147483648 | bytes 10485760
  71.3 1.0 copy.109
  72.4 3.6 %all-to-all-start.1 = ((bf16[16,2,32,512]{3,2,1,0:T(8,128)(2,1)}), bf16[16,2,32,512]{3,2,1,0:T(8,128)(2,1)S(1)}, u32[]{:S(2)}, u32[]{:S(2)}) async-start(bf16[16,2,32,512]{3,2,1,0:T(8,128)(2,1)} %copy.109), calls=%async_computation.1 | async-start | bytes 2097152 | tf_op jit(solution)/shard_map/all_to_all | solution.py:113
  75.9 5.3 %multiply_convert_fusion.1 = bf16[2,2048,512]{2,1,0:T(8,128)(2,1)S(1)} fusion(bf16[2,512,2048]{2,1,0:T(8,128)(2,1)} %get-tuple-element.14, bf16[2,512,512]{2,1,0:T(8,128)(2,1)S(1)} %bitcast.241), kind=kOutput, calls=%fused_computation.6 | convolution fusion | flops 2151677952 | bytes 9437184 | tf_op jit(solution)/shard_map/bth,bjt->bhj/dot_general | solution.py:97
  84.1 7.0 %fusion = bf16[2,2,2,2,2,2,32,2048]{7,6,5,4,3,2,0,1:T(8,128)(2,1)S(1)} fusion(bf16[2,2,2,2,2,32,512,1]{6,5,4,3,2,1,7,0:T(8,128)(2,1)S(1)} %fusion.16, bf16[1,2,512,2048]{3,2,1,0:T(8,128)(2,1)} %bitcast.247, bf16[1,2,512,2048]{3,2,1,0:T(8,128)(2,1)} %bitcast.246), kind=kOutput, calls=%fused_computation.1 | convolution fusion | flops 4307550208 | bytes 17825792 | tf_op jit(solution)/shard_map/bwyzcrt,gbth->gbwyzcrh/dot_general | solution.py:129
  91.8 1.9 slice_bitcast_fusion.4
  94.0 1.5 slice_bitcast_fusion.12
  95.5 3.6 %collective-permute-start.13 = (bf16[2,2,128,512]{3,2,0,1:T(8,128)(2,1)}, bf16[2,2,128,512]{3,2,0,1:T(8,128)(2,1)}, u32[]{:S(2)}, u32[]{:S(2)}) collective-permute-start(bf16[2,2,128,512]{3,2,0,1:T(8,128)(2,1)} %slice_bitcast_fusion.12), channel_id=1, source_target_pairs={{0,16},{16,0},{1,17},{17,1},{2,18},{18,2},{3,19},{19,3},{4,20},{20... | collective-permute-start | bytes 1572872 | tf_op jit(solution)/shard_map/ppermute | solution.py:44
  100.2 1.6 collective-permute-start.9
  101.8 1.7 slice_bitcast_fusion.2
  103.5 1.0 copy.110
  104.5 7.4 %collective-permute-done.13 = bf16[2,2,128,512]{3,2,0,1:T(8,128)(2,1)} collective-permute-done((bf16[2,2,128,512]{3,2,0,1:T(8,128)(2,1)}, bf16[2,2,128,512]{3,2,0,1:T(8,128)(2,1)}, u32[]{:S(2)}, u32[]{:S(2)}) %collective-permute-start.13) | collective-permute-done | bytes 524320 | tf_op jit(solution)/shard_map/ppermute | solution.py:44
  111.9 1.2 fusion.18
  113.1 1.7 collective-permute-start.14
  114.7 1.2 fusion.19
  116.0 3.3 %collective-permute-start.10 = (bf16[2,128,512]{2,1,0:T(8,128)(2,1)S(1)}, bf16[2,128,512]{2,1,0:T(8,128)(2,1)S(1)}, u32[]{:S(2)}, u32[]{:S(2)}) collective-permute-start(bf16[2,128,512]{2,1,0:T(8,128)(2,1)S(1)} %slice_bitcast_fusion.22), channel_id=1, source_target_pairs={{0,16},{16,0},{1,17},{17,1},{2,18},{18,2},{3,19},{19,3},{4,20},{20... | collective-permute-start | bytes 786440 | tf_op jit(solution)/shard_map/ppermute | solution.py:44
  119.3 1.9 collective-permute-done.14
  121.3 3.3 %collective-permute-start.15 = (bf16[128,512]{1,0:T(8,128)(2,1)S(1)}, bf16[128,512]{1,0:T(8,128)(2,1)}, u32[]{:S(2)}, u32[]{:S(2)}) collective-permute-start(bf16[128,512]{1,0:T(8,128)(2,1)S(1)} %slice_bitcast_fusion.28), channel_id=1, source_target_pairs={{0,64},{32,96},{64,0},{96,32},{1,65},{33,97},{65,1},{97,33},{2,66}... | collective-permute-start | bytes 393224 | tf_op jit(solution)/shard_map/ppermute | solution.py:44
  126.7 2.9 %collective-permute-start.11 = (bf16[128,512]{1,0:T(8,128)(2,1)}, bf16[128,512]{1,0:T(8,128)(2,1)}, u32[]{:S(2)}, u32[]{:S(2)}) collective-permute-start(bf16[128,512]{1,0:T(8,128)(2,1)} %slice_bitcast_fusion.30), channel_id=1, source_target_pairs={{0,64},{32,96},{64,0},{96,32},{1,65},{33,97},{65,1},{97,33},{2,66}... | collective-permute-start | bytes 393224 | tf_op jit(solution)/shard_map/ppermute | solution.py:44
  129.6 3.9 %fusion.7 = bf16[2,2,2,2,32,2048]{5,4,3,2,1,0:T(8,128)(2,1)} fusion(bf16[2,2,2,2,32,2048]{5,4,3,2,1,0:T(8,128)(2,1)} %collective-permute-done, bf16[2,2,2,2,2,32,2048]{6,5,4,3,2,1,0:T(8,128)(2,1)S(1)} %copy-done.3), kind=kLoop, calls=%fused_computation.17 | loop fusion | flops 4194304 | bytes 6291456 | tf_op jit(solution)/shard_map/convert_element_type | solution.py:134
  133.6 2.5 %fusion.6 = bf16[2,2,2,2,32,2048]{5,4,3,2,1,0:T(8,128)(2,1)S(1)} fusion(bf16[2,2,2,2,32,2048]{5,4,3,2,1,0:T(8,128)(2,1)} %collective-permute-done.1, bf16[2,2,2,2,2,32,2048]{6,5,4,3,2,1,0:T(8,128)(2,1)S(1)} %copy-done.1), kind=kLoop, calls=%fused_computation.15 | loop fusion | flops 4194304 | bytes 6291456 | tf_op jit(solution)/shard_map/convert_element_type | solution.py:135
  136.4 3.8 %fusion.35 = f32[2,512,512]{2,1,0:T(8,128)} fusion(bf16[2,512,2048]{2,1,0:T(8,128)(2,1)S(1)} %copy-done.9, bf16[2,512,2048]{2,1,0:T(8,128)(2,1)S(1)} %copy-done.5), kind=kOutput, calls=%fused_computation.117 | convolution fusion | flops 2147483648 | bytes 10485760 | tf_op jit(solution)/shard_map/bth,bih->bit/dot_general | solution.py:144
  140.1 7.0 %fusion.15 = bf16[2,512,512]{2,1,0:T(8,128)(2,1)S(1)} fusion(s32[2,512]{1,0:T(2,128)S(1)} %copy-done.8, f32[2,512,512]{2,1,0:T(8,128)} %fusion.35, bf16[2,512,2048]{2,1,0:T(8,128)(2,1)} %get-tuple-element.9, bf16[2,512,2048]{2,1,0:T(8,128)(2,1)} %param.9), kind=kOutput, calls=%fused_computation.41 | convolution fusion | flops 2686976000 | bytes 11538432 | tf_op jit(solution)/shard_map/bij,bit->bjt/dot_general | solution.py:148
  147.1 1.0 copy.163
  148.2 5.0 %all-to-all-start.2 = ((bf16[16,2,32,512]{3,2,1,0:T(8,128)(2,1)}), bf16[16,2,32,512]{3,2,1,0:T(8,128)(2,1)S(1)}, u32[]{:S(2)}, u32[]{:S(2)}) async-start(bf16[16,2,32,512]{3,2,1,0:T(8,128)(2,1)} %bitcast.234), calls=%async_computation.2 | async-start | bytes 2097152 | tf_op jit(solution)/shard_map/all_to_all | solution.py:153
  153.2 2.3 %slice_bitcast_fusion.11 = bf16[2,2,2,32,2048]{4,3,2,1,0:T(8,128)(2,1)} fusion(bf16[2,2,2,2,32,2048]{5,4,3,2,1,0:T(8,128)(2,1)} %fusion.7), kind=kLoop, calls=%fused_computation.60 | loop fusion | bytes 2097152 | tf_op jit(solution)/shard_map/squeeze | solution.py:44
  156.8 1.0 fusion.27
  157.9 1.1 slice_bitcast_fusion.10
  158.9 3.3 %collective-permute-start.5 = (bf16[2,2,2,32,2048]{4,3,2,1,0:T(8,128)(2,1)}, bf16[2,2,2,32,2048]{4,3,2,1,0:T(8,128)(2,1)}, u32[]{:S(2)}, u32[]{:S(2)}) collective-permute-start(bf16[2,2,2,32,2048]{4,3,2,1,0:T(8,128)(2,1)} %slice_bitcast_fusion.10), channel_id=1, source_target_pairs={{0,16},{16,0},{1,17},{17,1},{2,18},{18,2},{3,19},{19,3},{4,20},{20... | collective-permute-start | bytes 3145736 | tf_op jit(solution)/shard_map/ppermute | solution.py:44
  163.0 4.1 %all-to-all-done.2 = bf16[16,2,32,512]{3,2,1,0:T(8,128)(2,1)S(1)} async-done(((bf16[16,2,32,512]{3,2,1,0:T(8,128)(2,1)}), bf16[16,2,32,512]{3,2,1,0:T(8,128)(2,1)S(1)}, u32[]{:S(2)}, u32[]{:S(2)}) %all-to-all-start.2) | async-done | bytes 1048608 | tf_op jit(solution)/shard_map/all_to_all | solution.py:153
  167.1 1.0 copy.116
  168.2 10.5 %collective-permute-done.2 = bf16[2,2,2,32,2048]{4,3,2,1,0:T(8,128)(2,1)} collective-permute-done((bf16[2,2,2,32,2048]{4,3,2,1,0:T(8,128)(2,1)}, bf16[2,2,2,32,2048]{4,3,2,1,0:T(8,128)(2,1)}, u32[]{:S(2)}, u32[]{:S(2)}) %collective-permute-start.2) | collective-permute-done | bytes 1048608 | tf_op jit(solution)/shard_map/ppermute | solution.py:44
  178.7 1.9 fusion.11
  180.7 3.7 %collective-permute-start.3 = (bf16[2,2,32,2048]{3,2,1,0:T(8,128)(2,1)S(1)}, bf16[2,2,32,2048]{3,2,1,0:T(8,128)(2,1)S(1)}, u32[]{:S(2)}, u32[]{:S(2)}) collective-permute-start(bf16[2,2,32,2048]{3,2,1,0:T(8,128)(2,1)S(1)} %slice_bitcast_fusion.18), channel_id=1, source_target_pairs={{0,16},{16,0},{1,17},{17,1},{2,18},{18,2},{3,19},{19,3},{4,20},{20... | collective-permute-start | bytes 1572872 | tf_op jit(solution)/shard_map/ppermute | solution.py:44
  184.3 6.0 %collective-permute-done.5 = bf16[2,2,2,32,2048]{4,3,2,1,0:T(8,128)(2,1)} collective-permute-done((bf16[2,2,2,32,2048]{4,3,2,1,0:T(8,128)(2,1)}, bf16[2,2,2,32,2048]{4,3,2,1,0:T(8,128)(2,1)}, u32[]{:S(2)}, u32[]{:S(2)}) %collective-permute-start.5) | collective-permute-done | bytes 1048608 | tf_op jit(solution)/shard_map/ppermute | solution.py:44
  190.3 1.6 fusion.10
  192.1 8.5 %collective-permute-done.3 = bf16[2,2,32,2048]{3,2,1,0:T(8,128)(2,1)S(1)} collective-permute-done((bf16[2,2,32,2048]{3,2,1,0:T(8,128)(2,1)S(1)}, bf16[2,2,32,2048]{3,2,1,0:T(8,128)(2,1)S(1)}, u32[]{:S(2)}, u32[]{:S(2)}) %collective-permute-start.3) | collective-permute-done | bytes 524320 | tf_op jit(solution)/shard_map/ppermute | solution.py:44
  201.5 5.3 %collective-permute-done.6 = bf16[2,2,32,2048]{3,2,1,0:T(8,128)(2,1)S(1)} collective-permute-done((bf16[2,2,32,2048]{3,2,1,0:T(8,128)(2,1)S(1)}, bf16[2,2,32,2048]{3,2,1,0:T(8,128)(2,1)S(1)}, u32[]{:S(2)}, u32[]{:S(2)}) %collective-permute-start.6) | collective-permute-done | bytes 524320 | tf_op jit(solution)/shard_map/ppermute | solution.py:44
  207.1 4.5 %collective-permute-done.4 = bf16[2,32,2048]{2,1,0:T(8,128)(2,1)S(1)} collective-permute-done((bf16[2,32,2048]{2,1,0:T(8,128)(2,1)S(1)}, bf16[2,32,2048]{2,1,0:T(8,128)(2,1)S(1)}, u32[]{:S(2)}, u32[]{:S(2)}) %collective-permute-start.4) | collective-permute-done | bytes 262176 | tf_op jit(solution)/shard_map/ppermute | solution.py:44
  212.4 3.1 %collective-permute-done.7 = bf16[2,32,2048]{2,1,0:T(8,128)(2,1)S(1)} collective-permute-done((bf16[2,32,2048]{2,1,0:T(8,128)(2,1)S(1)}, bf16[2,32,2048]{2,1,0:T(8,128)(2,1)S(1)}, u32[]{:S(2)}, u32[]{:S(2)}) %collective-permute-start.7) | collective-permute-done | bytes 262176 | tf_op jit(solution)/shard_map/ppermute | solution.py:44
  (88 shorter events, 15.6 us)
Async XLA Ops:
  4.0 37.0 %all-to-all-start = ((bf16[2,2,16,32,512]{4,3,1,0,2:T(8,128)(2,1)}), bf16[2,2,16,32,512]{4,3,1,0,2:T(8,128)(2,1)S(1)}, u32[]{:S(2)}, u32[]{:S(2)}) async-start(bf16[2,2,16,32,512]{4,3,1,0,2:T(8,128)(2,1)} %copy.101), calls=%async_computation | async-start | bytes 4194304 | tf_op jit(solution)/shard_map/all_to_all | solution.py:69
  41.2 0.7 copy-start.8
  41.4 2.2 %copy-start.4 = (bf16[2,512,2048]{2,1,0:T(8,128)(2,1)S(1)}, bf16[2,512,2048]{2,1,0:T(8,128)(2,1)}, u32[]{:S(2)}) copy-start(bf16[2,512,2048]{2,1,0:T(8,128)(2,1)} %param.10) | copy-start | bytes 12582916
  43.6 2.4 %copy-start.6 = (bf16[2,512,2048]{2,1,0:T(8,128)(2,1)S(1)}, bf16[2,512,2048]{2,1,0:T(8,128)(2,1)}, u32[]{:S(2)}) copy-start(bf16[2,512,2048]{2,1,0:T(8,128)(2,1)} %param.9) | copy-start | bytes 12582916
  72.4 31.1 %all-to-all-start.1 = ((bf16[16,2,32,512]{3,2,1,0:T(8,128)(2,1)}), bf16[16,2,32,512]{3,2,1,0:T(8,128)(2,1)S(1)}, u32[]{:S(2)}, u32[]{:S(2)}) async-start(bf16[16,2,32,512]{3,2,1,0:T(8,128)(2,1)} %copy.109), calls=%async_computation.1 | async-start | bytes 2097152 | tf_op jit(solution)/shard_map/all_to_all | solution.py:113
  82.3 11.4 %collective-permute-start.12 = (bf16[2,2,2,128,512]{4,3,0,1,2:T(8,128)(2,1)S(1)}, bf16[2,2,2,128,512]{4,3,0,1,2:T(8,128)(2,1)S(1)}, u32[]{:S(2)}, u32[]{:S(2)}) collective-permute-start(bf16[2,2,2,128,512]{4,3,0,1,2:T(8,128)(2,1)S(1)} %bitcast.239), channel_id=1, source_target_pairs={{0,8},{8,0},{1,9},{9,1},{2,10},{10,2},{3,11},{11,3},{4,12},{12,4},... | collective-permute-start | bytes 3145736 | tf_op jit(solution)/shard_map/ppermute | solution.py:44
  82.4 16.6 %collective-permute-start.8 = (bf16[2,2,2,128,512]{4,3,2,1,0:T(8,128)(2,1)S(1)}, bf16[2,2,2,128,512]{4,3,2,1,0:T(8,128)(2,1)S(1)}, u32[]{:S(2)}, u32[]{:S(2)}) collective-permute-start(bf16[2,2,2,128,512]{4,3,2,1,0:T(8,128)(2,1)S(1)} %slice_bitcast_fusion.6), channel_id=1, source_target_pairs={{0,8},{8,0},{1,9},{9,1},{2,10},{10,2},{3,11},{11,3},{4,12},{12,4},... | collective-permute-start | bytes 3145736 | tf_op jit(solution)/shard_map/ppermute | solution.py:44
  91.8 3.7 %copy-start.2 = (bf16[2,2,2,2,2,32,2048]{6,5,4,3,2,1,0:T(8,128)(2,1)}, bf16[2,2,2,2,2,32,2048]{6,5,4,3,2,1,0:T(8,128)(2,1)S(1)}, u32[]{:S(2)}) copy-start(bf16[2,2,2,2,2,32,2048]{6,5,4,3,2,1,0:T(8,128)(2,1)S(1)} %get-tuple-element.17) | copy-start | bytes 12582916
  91.8 10.0 %copy-start = (bf16[2,2,2,2,2,32,2048]{6,5,4,3,2,1,0:T(8,128)(2,1)}, bf16[2,2,2,2,2,32,2048]{6,5,4,3,2,1,0:T(8,128)(2,1)S(1)}, u32[]{:S(2)}) copy-start(bf16[2,2,2,2,2,32,2048]{6,5,4,3,2,1,0:T(8,128)(2,1)S(1)} %get-tuple-element.16) | copy-start | bytes 12582916
  93.7 36.0 %collective-permute-start = (bf16[2,2,2,2,32,2048]{5,4,3,2,1,0:T(8,128)(2,1)}, bf16[2,2,2,2,32,2048]{5,4,3,2,1,0:T(8,128)(2,1)}, u32[]{:S(2)}, u32[]{:S(2)}) collective-permute-start(bf16[2,2,2,2,32,2048]{5,4,3,2,1,0:T(8,128)(2,1)} %slice_bitcast_fusion.4), channel_id=1, source_target_pairs={{0,8},{8,0},{1,9},{9,1},{2,10},{10,2},{3,11},{11,3},{4,12},{12,4},... | collective-permute-start | bytes 6291464 | tf_op jit(solution)/shard_map/ppermute | solution.py:44
  95.5 16.4 %collective-permute-start.13 = (bf16[2,2,128,512]{3,2,0,1:T(8,128)(2,1)}, bf16[2,2,128,512]{3,2,0,1:T(8,128)(2,1)}, u32[]{:S(2)}, u32[]{:S(2)}) collective-permute-start(bf16[2,2,128,512]{3,2,0,1:T(8,128)(2,1)} %slice_bitcast_fusion.12), channel_id=1, source_target_pairs={{0,16},{16,0},{1,17},{17,1},{2,18},{18,2},{3,19},{19,3},{4,20},{20... | collective-permute-start | bytes 1572872 | tf_op jit(solution)/shard_map/ppermute | solution.py:44
  100.2 14.5 %collective-permute-start.9 = (bf16[2,2,128,512]{3,2,1,0:T(8,128)(2,1)}, bf16[2,2,128,512]{3,2,1,0:T(8,128)(2,1)}, u32[]{:S(2)}, u32[]{:S(2)}) collective-permute-start(bf16[2,2,128,512]{3,2,1,0:T(8,128)(2,1)} %slice_bitcast_fusion.14), channel_id=1, source_target_pairs={{0,32},{32,0},{64,96},{96,64},{1,33},{33,1},{65,97},{97,65},{2,34}... | collective-permute-start | bytes 1572872 | tf_op jit(solution)/shard_map/ppermute | solution.py:44
  103.4 30.1 %collective-permute-start.1 = (bf16[2,2,2,2,32,2048]{5,4,3,2,1,0:T(8,128)(2,1)}, bf16[2,2,2,2,32,2048]{5,4,3,2,1,0:T(8,128)(2,1)}, u32[]{:S(2)}, u32[]{:S(2)}) collective-permute-start(bf16[2,2,2,2,32,2048]{5,4,3,2,1,0:T(8,128)(2,1)} %slice_bitcast_fusion.2), channel_id=1, source_target_pairs={{0,8},{8,0},{1,9},{9,1},{2,10},{10,2},{3,11},{11,3},{4,12},{12,4},... | collective-permute-start | bytes 6291464 | tf_op jit(solution)/shard_map/ppermute | solution.py:44
  103.5 26.2 %copy-start.3 = (bf16[2,2,2,2,2,32,2048]{6,5,4,3,2,1,0:T(8,128)(2,1)S(1)}, bf16[2,2,2,2,2,32,2048]{6,5,4,3,2,1,0:T(8,128)(2,1)}, u32[]{:S(2)}) copy-start(bf16[2,2,2,2,2,32,2048]{6,5,4,3,2,1,0:T(8,128)(2,1)} %copy-done.2) | copy-start | bytes 12582916
  113.1 8.1 %collective-permute-start.14 = (bf16[2,128,512]{2,1,0:T(8,128)(2,1)S(1)}, bf16[2,128,512]{2,1,0:T(8,128)(2,1)S(1)}, u32[]{:S(2)}, u32[]{:S(2)}) collective-permute-start(bf16[2,128,512]{2,1,0:T(8,128)(2,1)S(1)} %slice_bitcast_fusion.20), channel_id=1, source_target_pairs={{0,32},{32,0},{64,96},{96,64},{1,33},{33,1},{65,97},{97,65},{2,34}... | collective-permute-start | bytes 786440 | tf_op jit(solution)/shard_map/ppermute | solution.py:44
  115.9 17.6 %copy-start.1 = (bf16[2,2,2,2,2,32,2048]{6,5,4,3,2,1,0:T(8,128)(2,1)S(1)}, bf16[2,2,2,2,2,32,2048]{6,5,4,3,2,1,0:T(8,128)(2,1)}, u32[]{:S(2)}) copy-start(bf16[2,2,2,2,2,32,2048]{6,5,4,3,2,1,0:T(8,128)(2,1)} %copy-done) | copy-start | bytes 12582916
  116.0 9.3 %collective-permute-start.10 = (bf16[2,128,512]{2,1,0:T(8,128)(2,1)S(1)}, bf16[2,128,512]{2,1,0:T(8,128)(2,1)S(1)}, u32[]{:S(2)}, u32[]{:S(2)}) collective-permute-start(bf16[2,128,512]{2,1,0:T(8,128)(2,1)S(1)} %slice_bitcast_fusion.22), channel_id=1, source_target_pairs={{0,16},{16,0},{1,17},{17,1},{2,18},{18,2},{3,19},{19,3},{4,20},{20... | collective-permute-start | bytes 786440 | tf_op jit(solution)/shard_map/ppermute | solution.py:44
  121.3 34.6 %collective-permute-start.15 = (bf16[128,512]{1,0:T(8,128)(2,1)S(1)}, bf16[128,512]{1,0:T(8,128)(2,1)}, u32[]{:S(2)}, u32[]{:S(2)}) collective-permute-start(bf16[128,512]{1,0:T(8,128)(2,1)S(1)} %slice_bitcast_fusion.28), channel_id=1, source_target_pairs={{0,64},{32,96},{64,0},{96,32},{1,65},{33,97},{65,1},{97,33},{2,66}... | collective-permute-start | bytes 393224 | tf_op jit(solution)/shard_map/ppermute | solution.py:44
  125.4 0.7 copy-start.7
  126.7 30.1 %collective-permute-start.11 = (bf16[128,512]{1,0:T(8,128)(2,1)}, bf16[128,512]{1,0:T(8,128)(2,1)}, u32[]{:S(2)}, u32[]{:S(2)}) collective-permute-start(bf16[128,512]{1,0:T(8,128)(2,1)} %slice_bitcast_fusion.30), channel_id=1, source_target_pairs={{0,64},{32,96},{64,0},{96,32},{1,65},{33,97},{65,1},{97,33},{2,66}... | collective-permute-start | bytes 393224 | tf_op jit(solution)/shard_map/ppermute | solution.py:44
  129.6 6.5 %copy-start.9 = (bf16[2,512,2048]{2,1,0:T(8,128)(2,1)S(1)}, bf16[2,512,2048]{2,1,0:T(8,128)(2,1)}, u32[]{:S(2)}) copy-start(bf16[2,512,2048]{2,1,0:T(8,128)(2,1)} %get-tuple-element.10) | copy-start | bytes 12582916
  133.6 2.8 %copy-start.5 = (bf16[2,512,2048]{2,1,0:T(8,128)(2,1)S(1)}, bf16[2,512,2048]{2,1,0:T(8,128)(2,1)}, u32[]{:S(2)}) copy-start(bf16[2,512,2048]{2,1,0:T(8,128)(2,1)} %param.10) | copy-start | bytes 12582916
  148.2 19.0 %all-to-all-start.2 = ((bf16[16,2,32,512]{3,2,1,0:T(8,128)(2,1)}), bf16[16,2,32,512]{3,2,1,0:T(8,128)(2,1)S(1)}, u32[]{:S(2)}, u32[]{:S(2)}) async-start(bf16[16,2,32,512]{3,2,1,0:T(8,128)(2,1)} %bitcast.234), calls=%async_computation.2 | async-start | bytes 2097152 | tf_op jit(solution)/shard_map/all_to_all | solution.py:153
  155.5 23.2 %collective-permute-start.2 = (bf16[2,2,2,32,2048]{4,3,2,1,0:T(8,128)(2,1)}, bf16[2,2,2,32,2048]{4,3,2,1,0:T(8,128)(2,1)}, u32[]{:S(2)}, u32[]{:S(2)}) collective-permute-start(bf16[2,2,2,32,2048]{4,3,2,1,0:T(8,128)(2,1)} %slice_bitcast_fusion.11), channel_id=1, source_target_pairs={{0,32},{32,0},{64,96},{96,64},{1,33},{33,1},{65,97},{97,65},{2,34}... | collective-permute-start | bytes 3145736 | tf_op jit(solution)/shard_map/ppermute | solution.py:44
  158.9 31.4 %collective-permute-start.5 = (bf16[2,2,2,32,2048]{4,3,2,1,0:T(8,128)(2,1)}, bf16[2,2,2,32,2048]{4,3,2,1,0:T(8,128)(2,1)}, u32[]{:S(2)}, u32[]{:S(2)}) collective-permute-start(bf16[2,2,2,32,2048]{4,3,2,1,0:T(8,128)(2,1)} %slice_bitcast_fusion.10), channel_id=1, source_target_pairs={{0,16},{16,0},{1,17},{17,1},{2,18},{18,2},{3,19},{19,3},{4,20},{20... | collective-permute-start | bytes 3145736 | tf_op jit(solution)/shard_map/ppermute | solution.py:44
  180.7 19.9 %collective-permute-start.3 = (bf16[2,2,32,2048]{3,2,1,0:T(8,128)(2,1)S(1)}, bf16[2,2,32,2048]{3,2,1,0:T(8,128)(2,1)S(1)}, u32[]{:S(2)}, u32[]{:S(2)}) collective-permute-start(bf16[2,2,32,2048]{3,2,1,0:T(8,128)(2,1)S(1)} %slice_bitcast_fusion.18), channel_id=1, source_target_pairs={{0,16},{16,0},{1,17},{17,1},{2,18},{18,2},{3,19},{19,3},{4,20},{20... | collective-permute-start | bytes 1572872 | tf_op jit(solution)/shard_map/ppermute | solution.py:44
  192.0 14.8 %collective-permute-start.6 = (bf16[2,2,32,2048]{3,2,1,0:T(8,128)(2,1)S(1)}, bf16[2,2,32,2048]{3,2,1,0:T(8,128)(2,1)S(1)}, u32[]{:S(2)}, u32[]{:S(2)}) collective-permute-start(bf16[2,2,32,2048]{3,2,1,0:T(8,128)(2,1)S(1)} %slice_bitcast_fusion.16), channel_id=1, source_target_pairs={{0,32},{32,0},{64,96},{96,64},{1,33},{33,1},{65,97},{97,65},{2,34}... | collective-permute-start | bytes 1572872 | tf_op jit(solution)/shard_map/ppermute | solution.py:44
  200.8 10.8 %collective-permute-start.4 = (bf16[2,32,2048]{2,1,0:T(8,128)(2,1)S(1)}, bf16[2,32,2048]{2,1,0:T(8,128)(2,1)S(1)}, u32[]{:S(2)}, u32[]{:S(2)}) collective-permute-start(bf16[2,32,2048]{2,1,0:T(8,128)(2,1)S(1)} %slice_bitcast_fusion.26), channel_id=1, source_target_pairs={{0,64},{32,96},{64,0},{96,32},{1,65},{33,97},{65,1},{97,33},{2,66}... | collective-permute-start | bytes 786440 | tf_op jit(solution)/shard_map/ppermute | solution.py:44
  207.0 8.5 %collective-permute-start.7 = (bf16[2,32,2048]{2,1,0:T(8,128)(2,1)S(1)}, bf16[2,32,2048]{2,1,0:T(8,128)(2,1)S(1)}, u32[]{:S(2)}, u32[]{:S(2)}) collective-permute-start(bf16[2,32,2048]{2,1,0:T(8,128)(2,1)S(1)} %slice_bitcast_fusion.24), channel_id=1, source_target_pairs={{0,64},{32,96},{64,0},{96,32},{1,65},{33,97},{65,1},{97,33},{2,66}... | collective-permute-start | bytes 786440 | tf_op jit(solution)/shard_map/ppermute | solution.py:44
where the time goes:
time: 218 us; the launch traced here: 216 us
  waiting for transfers between devices  77 us (35%)
  matrix products  51.1 us (23%)
  starting transfers between devices  39.6 us (18%)
  local copies, waits for them, and re-layouts  26.6 us (12%)
  other arithmetic  20.8 us (10%)
    ppermute x16, waiting for transfers between devices, tree_reduce(): lax.ppermute(lax.index_in_dim(acc, 1, axis, keepdims=False), name, perm=p...  47.9 us
    ppermute x16, starting transfers between devices, tree_reduce(): lax.ppermute(lax.index_in_dim(acc, 1, axis, keepdims=False), name, perm=p...  25.3 us
    all_to_all x1, waiting for transfers between devices, local(): both = lax.all_to_all(both, 'mp', split_axis=2, concat_axis=1, tiled=True)  25 us
    dot_general x1, matrix products, local(): jnp.einsum('sbkt,bhsk->bth', cot_blocks, down_view, preferred_element_typ...  13.4 us
    squeeze x15, local copies, waits for them, and re-layouts, tree_reduce(): lax.index_in_dim(acc, 1, axis, keepdims=False)  10.1 us
    unnamed x37, local copies, waits for them, and re-layouts  8.93 us
    dot_general x1, matrix products, local(): jnp.einsum('bwyzcrt,gbth->gbwyzcrh', feat_l, d_both, preferred_element_ty...  7.02 us
    dot_general x1, matrix products, local(): jnp.einsum('bij,bit->bjt', onehot, d_mixed_p, preferred_element_type=jnp....  6.97 us
  transfers between devices with their start and end apart: 19, of which 11 were waited for; matrix products, arithmetic and copies ran while one was open for 29% of the time, Pallas kernels for 0%

commit v1 on v0

--- a/solution.py
+++ b/solution.py
@@ -65,10 +65,13 @@
     s_here = features.shape[0] // (block_total * piece)
     grad_scale = (tok_count * n_dp) ** (-0.5)
 
-    both = jnp.stack([features, cotangent]).reshape(2, s_here, block_total, piece, tok_count)
-    both = lax.all_to_all(both, "mp", split_axis=2, concat_axis=1, tiled=True)
-    feat_blocks = both[0]
-    cot_blocks = both[1]
+    local_shape = (s_here, block_total, piece, tok_count)
+    feat_blocks = lax.all_to_all(
+        features.reshape(local_shape), "mp", split_axis=1, concat_axis=0, tiled=True
+    )
+    cot_blocks = lax.all_to_all(
+        cotangent.reshape(local_shape), "mp", split_axis=1, concat_axis=0, tiled=True
+    )
 
     onehot = perm_matrix(block_perm)
     feat_rows = feat_blocks.transpose(1, 0, 2, 3).reshape(blocks_here, inner, tok_count)
@@ -150,9 +153,9 @@
     ).astype(jnp.bfloat16)
     d_mixed = d_mixed.reshape(blocks_here, block_total, piece, tok_count).transpose(1, 0, 2, 3)
 
-    d_features = lax.all_to_all(d_mixed, "mp", split_axis=0, concat_axis=1, tiled=True).reshape(
-        features.shape
-    )
+    d_features = lax.all_to_all(
+        d_mixed, "mp", split_axis=0, concat_axis=1, tiled=True
+    ).reshape(features.shape)
     return (outputs, d_features, gate_grad, up_grad, down_grad)
 
 

time: 218 us -> 208 us (0.954)
  waiting for transfers between devices: 77 us -> 62.3 us
  starting transfers between devices: 39.6 us -> 44 us
    all_to_all x1 -> x2, waiting for transfers between devices: 25 us -> 9.94 us  [the longest x1 8.57 us: local(): lax.all_to_all(features.reshape(local_shape), 'mp', split_axis=1, concat_...]
    all_to_all x1 -> x2, starting transfers between devices: 5.77 us -> 9.32 us  [the longest x1 5.77 us: local(): lax.all_to_all(features.reshape(local_shape), 'mp', split_axis=1, concat_...]
    unnamed x1, matrix products: 5.84 us -> 2.37 us
    reshape x0 -> x2, local copies, waits for them, and re-layouts: none -> 3.44 us  [the longest x1 2.39 us: local(): features.reshape(local_shape)]
    dot_general x1, matrix products: 2.39 us -> 5.68 us  [local(): jnp.einsum('bit,bih->bth', feat_p, w_up, preferred_element_type=jnp.float32)]
    unnamed x37 -> x47, local copies, waits for them, and re-layouts: 8.93 us -> 9.1 us
  transfers between devices with their start and end apart: 19 -> 20, of which waited for: 11 -> 12; matrix products, arithmetic and copies ran while one was open for 29% -> 36% of each run, Pallas kernels for 0% -> 0%
where the time goes in v1:
time: 208 us; the launch traced here: 206 us
  waiting for transfers between devices  62.3 us (30%)
  matrix products  51.8 us (25%)
  starting transfers between devices  44 us (21%)
  local copies, waits for them, and re-layouts  28 us (13%)
  other arithmetic  19.1 us (9%)
    ppermute x16, waiting for transfers between devices, tree_reduce(): lax.ppermute(lax.index_in_dim(acc, 1, axis, keepdims=False), name, perm=p...  48.2 us
    ppermute x16, starting transfers between devices, tree_reduce(): lax.ppermute(lax.index_in_dim(acc, 1, axis, keepdims=False), name, perm=p...  25.3 us
    dot_general x1, matrix products, local(): jnp.einsum('sbkt,bhsk->bth', cot_blocks, down_view, preferred_element_typ...  14.4 us
    squeeze x15, local copies, waits for them, and re-layouts, tree_reduce(): lax.index_in_dim(acc, 1, axis, keepdims=False)  9.97 us
    unnamed x47, local copies, waits for them, and re-layouts  9.1 us
    all_to_all x1, waiting for transfers between devices, local(): lax.all_to_all(features.reshape(local_shape), 'mp', split_axis=1, concat_...  8.57 us
    dot_general x1, matrix products, local(): jnp.einsum('bwyzcrt,gbth->gbwyzcrh', feat_l, d_both, preferred_element_ty...  7.02 us
    dot_general x1, matrix products, local(): jnp.einsum('bij,bit->bjt', onehot, d_mixed_p, preferred_element_type=jnp....  6.97 us
  transfers between devices with their start and end apart: 20, of which 12 were waited for; matrix products, arithmetic and copies ran while one was open for 36% of the time, Pallas kernels for 0%

profile of v1, /device:TPU:0, one launch (start us, length us, event | category | flops | bytes accessed | tf_op | source)
XLA Modules:
  0.0 206.5 jit_solution(4880478375289768401)
XLA Ops:
  0.6 2.4 %copy.78 = bf16[2,16,32,512]{3,2,0,1:T(8,128)(2,1)} copy(bf16[2,16,32,512]{3,2,1,0:T(8,128)(2,1)} %bitcast.241) | data formatting | bytes 2097152 | tf_op jit(solution)/shard_map/reshape | solution.py:70
  3.0 5.8 %all-to-all-start = ((bf16[2,16,32,512]{3,2,0,1:T(8,128)(2,1)}), bf16[2,16,32,512]{3,2,0,1:T(8,128)(2,1)S(1)}, u32[]{:S(2)}, u32[]{:S(2)}) async-start(bf16[2,16,32,512]{3,2,0,1:T(8,128)(2,1)} %copy.78), calls=%async_computation | async-start | bytes 2097152 | tf_op jit(solution)/shard_map/all_to_all | solution.py:69
  8.8 1.0 copy.86
  9.9 6.3 %copy.83 = bf16[2,2048,512]{1,2,0:T(8,128)(2,1)} copy(bf16[2,2048,512]{2,1,0:T(8,128)(2,1)} %param.11) | data formatting | bytes 8388608 | tf_op args[5]
  16.1 8.6 %all-to-all-done = bf16[2,16,32,512]{3,2,0,1:T(8,128)(2,1)S(1)} async-done(((bf16[2,16,32,512]{3,2,0,1:T(8,128)(2,1)}), bf16[2,16,32,512]{3,2,0,1:T(8,128)(2,1)S(1)}, u32[]{:S(2)}, u32[]{:S(2)}) %all-to-all-start) | async-done | bytes 1048608 | tf_op jit(solution)/shard_map/all_to_all | solution.py:69
  24.7 3.6 %all-to-all-start.2 = ((bf16[2,16,32,512]{3,2,0,1:T(8,128)(2,1)}), bf16[2,16,32,512]{3,2,0,1:T(8,128)(2,1)S(1)}, u32[]{:S(2)}, u32[]{:S(2)}) async-start(bf16[2,16,32,512]{3,2,0,1:T(8,128)(2,1)} %copy.86), calls=%async_computation.2 | async-start | bytes 2097152 | tf_op jit(solution)/shard_map/all_to_all | solution.py:72
  29.1 1.3 copy-done.5
  30.5 5.7 %fusion.32 = f32[2,512,2048]{2,1,0:T(8,128)} fusion(bf16[2,512,512]{2,1,0:T(8,128)(2,1)S(1)} %fusion.14, bf16[2,512,2048]{2,1,0:T(8,128)(2,1)S(1)} %copy-done.5), kind=kOutput, calls=%fused_computation.113 | convolution fusion | flops 2147483648 | bytes 13631488 | tf_op jit(solution)/shard_map/bit,bih->bth/dot_general | solution.py:87
  36.2 5.6 %fusion.31 = f32[2,512,2048]{2,1,0:T(8,128)} fusion(bf16[2,512,512]{2,1,0:T(8,128)(2,1)S(1)} %fusion.14, bf16[2,512,2048]{2,1,0:T(8,128)(2,1)S(1)} %copy-done.7), kind=kOutput, calls=%fused_computation.112 | convolution fusion | flops 2147483648 | bytes 13631488 | tf_op jit(solution)/shard_map/bit,bih->bth/dot_general | solution.py:83
  41.8 1.4 all-to-all-done.2
  43.3 14.4 %multiply_convert_fusion.3 = (bf16[2,512,2048]{2,1,0:T(8,128)(2,1)}, bf16[2,512,2048]{2,1,0:T(8,128)(2,1)S(1)}, bf16[2,512,2048]{2,1,0:T(8,128)(2,1)}) fusion(f32[2,512,2048]{2,1,0:T(8,128)} %fusion.32, f32[2,512,2048]{2,1,0:T(8,128)} %fusion.31, bf16[16,2,32,512]{3,2,0,1:T(8,128)(2,1)S(1)} %bitcast.246, bf16[2,2048,16,32]{1,3,2,0:T(8,128)(2,1)} %bitcast.234), kind=kOutput, calls=%fused_computation.8 | convolution fusion | flops 2185232384 | bytes 34603008 | tf_op jit(solution)/shard_map/sbkt,bhsk->bth/dot_general | solution.py:121
  57.7 2.4 %fusion.33 = f32[2,512,512]{1,2,0:S(1)} fusion(bf16[2,512,2048]{2,1,0:T(8,128)(2,1)S(1)} %get-tuple-element.14, bf16[2,2048,512]{2,1,0:T(8,128)(2,1)S(1)} %copy-done.4), kind=kOutput, calls=%fused_computation.114 | convolution fusion | flops 2147483648 | bytes 10485760
  61.4 4.3 %all-to-all-start.1 = ((bf16[16,2,32,512]{3,2,1,0:T(8,128)(2,1)}), bf16[16,2,32,512]{3,2,1,0:T(8,128)(2,1)S(1)}, u32[]{:S(2)}, u32[]{:S(2)}) async-start(bf16[16,2,32,512]{3,2,1,0:T(8,128)(2,1)} %copy.84), calls=%async_computation.1 | async-start | bytes 2097152 | tf_op jit(solution)/shard_map/all_to_all | solution.py:116
  65.7 5.3 %multiply_convert_fusion.1 = bf16[2,2048,512]{2,1,0:T(8,128)(2,1)S(1)} fusion(bf16[2,512,2048]{2,1,0:T(8,128)(2,1)} %copy-done.14, bf16[2,512,512]{2,1,0:T(8,128)(2,1)S(1)} %bitcast.247), kind=kOutput, calls=%fused_computation.6 | convolution fusion | flops 2151677952 | bytes 9437184 | tf_op jit(solution)/shard_map/bth,bjt->bhj/dot_general | solution.py:100
  73.9 7.0 %fusion = bf16[2,2,2,2,2,2,32,2048]{7,6,5,4,3,2,0,1:T(8,128)(2,1)S(1)} fusion(bf16[2,2,2,2,2,32,512,1]{6,5,4,3,2,1,7,0:T(8,128)(2,1)S(1)} %fusion.16, bf16[1,2,512,2048]{3,2,1,0:T(8,128)(2,1)} %bitcast.251, bf16[1,2,512,2048]{3,2,1,0:T(8,128)(2,1)} %bitcast.250), kind=kOutput, calls=%fused_computation.1 | convolution fusion | flops 4307550208 | bytes 17825792 | tf_op jit(solution)/shard_map/bwyzcrt,gbth->gbwyzcrh/dot_general | solution.py:132
  81.6 1.7 slice_bitcast_fusion.4
  83.7 1.6 slice_bitcast_fusion.12
  85.3 3.5 %collective-permute-start.13 = (bf16[2,2,128,512]{3,2,0,1:T(8,128)(2,1)}, bf16[2,2,128,512]{3,2,0,1:T(8,128)(2,1)}, u32[]{:S(2)}, u32[]{:S(2)}) collective-permute-start(bf16[2,2,128,512]{3,2,0,1:T(8,128)(2,1)} %slice_bitcast_fusion.12), channel_id=1, source_target_pairs={{0,16},{16,0},{1,17},{17,1},{2,18},{18,2},{3,19},{19,3},{4,20},{20... | collective-permute-start | bytes 1572872 | tf_op jit(solution)/shard_map/ppermute | solution.py:44
  89.9 1.6 collective-permute-start.9
  91.5 1.6 slice_bitcast_fusion.2
  93.1 1.0 copy.85
  94.1 7.6 %collective-permute-done.13 = bf16[2,2,128,512]{3,2,0,1:T(8,128)(2,1)} collective-permute-done((bf16[2,2,128,512]{3,2,0,1:T(8,128)(2,1)}, bf16[2,2,128,512]{3,2,0,1:T(8,128)(2,1)}, u32[]{:S(2)}, u32[]{:S(2)}) %collective-permute-start.13) | collective-permute-done | bytes 524320 | tf_op jit(solution)/shard_map/ppermute | solution.py:44
  101.7 1.2 fusion.18
  102.9 1.6 collective-permute-start.14
  104.6 1.2 fusion.19
  105.8 3.3 %collective-permute-start.10 = (bf16[2,128,512]{2,1,0:T(8,128)(2,1)S(1)}, bf16[2,128,512]{2,1,0:T(8,128)(2,1)S(1)}, u32[]{:S(2)}, u32[]{:S(2)}) collective-permute-start(bf16[2,128,512]{2,1,0:T(8,128)(2,1)S(1)} %slice_bitcast_fusion.22), channel_id=1, source_target_pairs={{0,16},{16,0},{1,17},{17,1},{2,18},{18,2},{3,19},{19,3},{4,20},{20... | collective-permute-start | bytes 786440 | tf_op jit(solution)/shard_map/ppermute | solution.py:44
  109.1 2.1 %collective-permute-done.14 = bf16[2,128,512]{2,1,0:T(8,128)(2,1)S(1)} collective-permute-done((bf16[2,128,512]{2,1,0:T(8,128)(2,1)S(1)}, bf16[2,128,512]{2,1,0:T(8,128)(2,1)S(1)}, u32[]{:S(2)}, u32[]{:S(2)}) %collective-permute-start.14) | collective-permute-done | bytes 262176 | tf_op jit(solution)/shard_map/ppermute | solution.py:44
  111.3 3.3 %collective-permute-start.15 = (bf16[128,512]{1,0:T(8,128)(2,1)S(1)}, bf16[128,512]{1,0:T(8,128)(2,1)}, u32[]{:S(2)}, u32[]{:S(2)}) collective-permute-start(bf16[128,512]{1,0:T(8,128)(2,1)S(1)} %slice_bitcast_fusion.28), channel_id=1, source_target_pairs={{0,64},{32,96},{64,0},{96,32},{1,65},{33,97},{65,1},{97,33},{2,66}... | collective-permute-start | bytes 393224 | tf_op jit(solution)/shard_map/ppermute | solution.py:44
  116.7 2.9 %collective-permute-start.11 = (bf16[128,512]{1,0:T(8,128)(2,1)}, bf16[128,512]{1,0:T(8,128)(2,1)}, u32[]{:S(2)}, u32[]{:S(2)}) collective-permute-start(bf16[128,512]{1,0:T(8,128)(2,1)} %slice_bitcast_fusion.30), channel_id=1, source_target_pairs={{0,64},{32,96},{64,0},{96,32},{1,65},{33,97},{65,1},{97,33},{2,66}... | collective-permute-start | bytes 393224 | tf_op jit(solution)/shard_map/ppermute | solution.py:44
  119.7 3.9 %fusion.7 = bf16[2,2,2,2,32,2048]{5,4,3,2,1,0:T(8,128)(2,1)} fusion(bf16[2,2,2,2,32,2048]{5,4,3,2,1,0:T(8,128)(2,1)} %collective-permute-done, bf16[2,2,2,2,2,32,2048]{6,5,4,3,2,1,0:T(8,128)(2,1)S(1)} %copy-done.3), kind=kLoop, calls=%fused_computation.17 | loop fusion | flops 4194304 | bytes 6291456 | tf_op jit(solution)/shard_map/convert_element_type | solution.py:137
  123.6 2.5 %fusion.6 = bf16[2,2,2,2,32,2048]{5,4,3,2,1,0:T(8,128)(2,1)S(1)} fusion(bf16[2,2,2,2,32,2048]{5,4,3,2,1,0:T(8,128)(2,1)} %collective-permute-done.1, bf16[2,2,2,2,2,32,2048]{6,5,4,3,2,1,0:T(8,128)(2,1)S(1)} %copy-done.1), kind=kLoop, calls=%fused_computation.15 | loop fusion | flops 4194304 | bytes 6291456 | tf_op jit(solution)/shard_map/convert_element_type | solution.py:138
  126.4 3.7 %fusion.34 = f32[2,512,512]{2,1,0:T(8,128)} fusion(bf16[2,512,2048]{2,1,0:T(8,128)(2,1)S(1)} %copy-done.13, bf16[2,512,2048]{2,1,0:T(8,128)(2,1)S(1)} %copy-done.6), kind=kOutput, calls=%fused_computation.115 | convolution fusion | flops 2147483648 | bytes 10485760 | tf_op jit(solution)/shard_map/bth,bih->bit/dot_general | solution.py:147
  130.1 7.0 %fusion.15 = bf16[2,512,512]{2,1,0:T(8,128)(2,1)S(1)} fusion(s32[2,512]{1,0:T(2,128)S(1)} %copy-done.12, f32[2,512,512]{2,1,0:T(8,128)} %fusion.34, bf16[2,512,2048]{2,1,0:T(8,128)(2,1)} %get-tuple-element.9, bf16[2,512,2048]{2,1,0:T(8,128)(2,1)} %param.9), kind=kOutput, calls=%fused_computation.40 | convolution fusion | flops 2686976000 | bytes 11538432 | tf_op jit(solution)/shard_map/bij,bit->bjt/dot_general | solution.py:151
  137.1 1.0 copy.141
  138.1 5.1 %all-to-all-start.3 = ((bf16[16,2,32,512]{3,2,1,0:T(8,128)(2,1)}), bf16[16,2,32,512]{3,2,1,0:T(8,128)(2,1)S(1)}, u32[]{:S(2)}, u32[]{:S(2)}) async-start(bf16[16,2,32,512]{3,2,1,0:T(8,128)(2,1)} %bitcast.238), calls=%async_computation.3 | async-start | bytes 2097152 | tf_op jit(solution)/shard_map/all_to_all | solution.py:156
  143.2 2.3 %slice_bitcast_fusion.11 = bf16[2,2,2,32,2048]{4,3,2,1,0:T(8,128)(2,1)} fusion(bf16[2,2,2,2,32,2048]{5,4,3,2,1,0:T(8,128)(2,1)} %fusion.7), kind=kLoop, calls=%fused_computation.59 | loop fusion | bytes 2097152 | tf_op jit(solution)/shard_map/squeeze | solution.py:44
  147.9 1.1 slice_bitcast_fusion.10
  149.0 3.3 %collective-permute-start.5 = (bf16[2,2,2,32,2048]{4,3,2,1,0:T(8,128)(2,1)}, bf16[2,2,2,32,2048]{4,3,2,1,0:T(8,128)(2,1)}, u32[]{:S(2)}, u32[]{:S(2)}) collective-permute-start(bf16[2,2,2,32,2048]{4,3,2,1,0:T(8,128)(2,1)} %slice_bitcast_fusion.10), channel_id=1, source_target_pairs={{0,16},{16,0},{1,17},{17,1},{2,18},{18,2},{3,19},{19,3},{4,20},{20... | collective-permute-start | bytes 3145736 | tf_op jit(solution)/shard_map/ppermute | solution.py:44
  153.1 4.2 %all-to-all-done.3 = bf16[16,2,32,512]{3,2,1,0:T(8,128)(2,1)S(1)} async-done(((bf16[16,2,32,512]{3,2,1,0:T(8,128)(2,1)}), bf16[16,2,32,512]{3,2,1,0:T(8,128)(2,1)S(1)}, u32[]{:S(2)}, u32[]{:S(2)}) %all-to-all-start.3) | async-done | bytes 1048608 | tf_op jit(solution)/shard_map/all_to_all | solution.py:156
  158.4 10.6 %collective-permute-done.2 = bf16[2,2,2,32,2048]{4,3,2,1,0:T(8,128)(2,1)} collective-permute-done((bf16[2,2,2,32,2048]{4,3,2,1,0:T(8,128)(2,1)}, bf16[2,2,2,32,2048]{4,3,2,1,0:T(8,128)(2,1)}, u32[]{:S(2)}, u32[]{:S(2)}) %collective-permute-start.2) | collective-permute-done | bytes 1048608 | tf_op jit(solution)/shard_map/ppermute | solution.py:44
  168.9 1.9 fusion.11
  170.9 3.7 %collective-permute-start.3 = (bf16[2,2,32,2048]{3,2,1,0:T(8,128)(2,1)S(1)}, bf16[2,2,32,2048]{3,2,1,0:T(8,128)(2,1)S(1)}, u32[]{:S(2)}, u32[]{:S(2)}) collective-permute-start(bf16[2,2,32,2048]{3,2,1,0:T(8,128)(2,1)S(1)} %slice_bitcast_fusion.18), channel_id=1, source_target_pairs={{0,16},{16,0},{1,17},{17,1},{2,18},{18,2},{3,19},{19,3},{4,20},{20... | collective-permute-start | bytes 1572872 | tf_op jit(solution)/shard_map/ppermute | solution.py:44
  174.6 6.0 %collective-permute-done.5 = bf16[2,2,2,32,2048]{4,3,2,1,0:T(8,128)(2,1)} collective-permute-done((bf16[2,2,2,32,2048]{4,3,2,1,0:T(8,128)(2,1)}, bf16[2,2,2,32,2048]{4,3,2,1,0:T(8,128)(2,1)}, u32[]{:S(2)}, u32[]{:S(2)}) %collective-permute-start.5) | collective-permute-done | bytes 1048608 | tf_op jit(solution)/shard_map/ppermute | solution.py:44
  180.6 1.6 fusion.10
  182.5 8.4 %collective-permute-done.3 = bf16[2,2,32,2048]{3,2,1,0:T(8,128)(2,1)S(1)} collective-permute-done((bf16[2,2,32,2048]{3,2,1,0:T(8,128)(2,1)S(1)}, bf16[2,2,32,2048]{3,2,1,0:T(8,128)(2,1)S(1)}, u32[]{:S(2)}, u32[]{:S(2)}) %collective-permute-start.3) | collective-permute-done | bytes 524320 | tf_op jit(solution)/shard_map/ppermute | solution.py:44
  191.7 5.4 %collective-permute-done.6 = bf16[2,2,32,2048]{3,2,1,0:T(8,128)(2,1)S(1)} collective-permute-done((bf16[2,2,32,2048]{3,2,1,0:T(8,128)(2,1)S(1)}, bf16[2,2,32,2048]{3,2,1,0:T(8,128)(2,1)S(1)}, u32[]{:S(2)}, u32[]{:S(2)}) %collective-permute-start.6) | collective-permute-done | bytes 524320 | tf_op jit(solution)/shard_map/ppermute | solution.py:44
  197.3 4.4 %collective-permute-done.4 = bf16[2,32,2048]{2,1,0:T(8,128)(2,1)S(1)} collective-permute-done((bf16[2,32,2048]{2,1,0:T(8,128)(2,1)S(1)}, bf16[2,32,2048]{2,1,0:T(8,128)(2,1)S(1)}, u32[]{:S(2)}, u32[]{:S(2)}) %collective-permute-start.4) | collective-permute-done | bytes 262176 | tf_op jit(solution)/shard_map/ppermute | solution.py:44
  202.6 3.0 %collective-permute-done.7 = bf16[2,32,2048]{2,1,0:T(8,128)(2,1)S(1)} collective-permute-done((bf16[2,32,2048]{2,1,0:T(8,128)(2,1)S(1)}, bf16[2,32,2048]{2,1,0:T(8,128)(2,1)S(1)}, u32[]{:S(2)}, u32[]{:S(2)}) %collective-permute-start.7) | collective-permute-done | bytes 262176 | tf_op jit(solution)/shard_map/ppermute | solution.py:44
  (97 shorter events, 17.0 us)
Async XLA Ops:
  0.6 8.2 %copy-start.9 = (bf16[1024,512]{1,0:T(8,128)(2,1)S(1)}, bf16[1024,512]{1,0:T(8,128)(2,1)}, u32[]{:S(2)}) copy-start(bf16[1024,512]{1,0:T(8,128)(2,1)} %param.7) | copy-start | bytes 3145732
  3.0 21.7 %all-to-all-start = ((bf16[2,16,32,512]{3,2,0,1:T(8,128)(2,1)}), bf16[2,16,32,512]{3,2,0,1:T(8,128)(2,1)S(1)}, u32[]{:S(2)}, u32[]{:S(2)}) async-start(bf16[2,16,32,512]{3,2,0,1:T(8,128)(2,1)} %copy.78), calls=%async_computation | async-start | bytes 2097152 | tf_op jit(solution)/shard_map/all_to_all | solution.py:69
  16.1 12.2 %copy-start.12 = (s32[2,512]{1,0:T(2,128)S(1)}, s32[2,512]{1,0:T(2,128)}, u32[]{:S(2)}) copy-start(s32[2,512]{1,0:T(2,128)} %param.8) | copy-start | bytes 12292
  24.7 18.5 %all-to-all-start.2 = ((bf16[2,16,32,512]{3,2,0,1:T(8,128)(2,1)}), bf16[2,16,32,512]{3,2,0,1:T(8,128)(2,1)S(1)}, u32[]{:S(2)}, u32[]{:S(2)}) async-start(bf16[2,16,32,512]{3,2,0,1:T(8,128)(2,1)} %copy.86), calls=%async_computation.2 | async-start | bytes 2097152 | tf_op jit(solution)/shard_map/all_to_all | solution.py:72
  28.3 2.2 %copy-start.5 = (bf16[2,512,2048]{2,1,0:T(8,128)(2,1)S(1)}, bf16[2,512,2048]{2,1,0:T(8,128)(2,1)}, u32[]{:S(2)}) copy-start(bf16[2,512,2048]{2,1,0:T(8,128)(2,1)} %param.10) | copy-start | bytes 12582916
  30.5 5.7 %copy-start.7 = (bf16[2,512,2048]{2,1,0:T(8,128)(2,1)S(1)}, bf16[2,512,2048]{2,1,0:T(8,128)(2,1)}, u32[]{:S(2)}) copy-start(bf16[2,512,2048]{2,1,0:T(8,128)(2,1)} %param.9) | copy-start | bytes 12582916
  43.3 14.4 %copy-start.10 = (bf16[8,2,2,32,512]{4,3,1,0,2:T(8,128)(2,1)}, bf16[8,2,2,32,512]{4,3,1,0,2:T(8,128)(2,1)S(1)}, u32[]{:S(2)}) copy-start(bf16[8,2,2,32,512]{4,3,1,0,2:T(8,128)(2,1)S(1)} %copy.88) | copy-start | bytes 3145732
  43.3 14.4 %copy-start.4 = (bf16[2,2048,512]{2,1,0:T(8,128)(2,1)S(1)}, bf16[2,2048,512]{2,1,0:T(8,128)(2,1)}, u32[]{:S(2)}) copy-start(bf16[2,2048,512]{2,1,0:T(8,128)(2,1)} %param.11) | copy-start | bytes 12582916
  57.7 2.4 %copy-start.14 = (bf16[2,512,2048]{2,1,0:T(8,128)(2,1)}, bf16[2,512,2048]{2,1,0:T(8,128)(2,1)S(1)}, u32[]{:S(2)}) copy-start(bf16[2,512,2048]{2,1,0:T(8,128)(2,1)S(1)} %get-tuple-element.14) | copy-start | bytes 12582916
  60.1 5.6 %copy-start.11 = (bf16[8,2,2,32,512]{4,3,1,0,2:T(8,128)(2,1)S(1)}, bf16[8,2,2,32,512]{4,3,1,0,2:T(8,128)(2,1)}, u32[]{:S(2)}) copy-start(bf16[8,2,2,32,512]{4,3,1,0,2:T(8,128)(2,1)} %copy-done.10) | copy-start | bytes 3145732
  61.4 31.6 %all-to-all-start.1 = ((bf16[16,2,32,512]{3,2,1,0:T(8,128)(2,1)}), bf16[16,2,32,512]{3,2,1,0:T(8,128)(2,1)S(1)}, u32[]{:S(2)}, u32[]{:S(2)}) async-start(bf16[16,2,32,512]{3,2,1,0:T(8,128)(2,1)} %copy.84), calls=%async_computation.1 | async-start | bytes 2097152 | tf_op jit(solution)/shard_map/all_to_all | solution.py:116
  72.1 11.3 %collective-permute-start.12 = (bf16[2,2,2,128,512]{4,3,0,1,2:T(8,128)(2,1)S(1)}, bf16[2,2,2,128,512]{4,3,0,1,2:T(8,128)(2,1)S(1)}, u32[]{:S(2)}, u32[]{:S(2)}) collective-permute-start(bf16[2,2,2,128,512]{4,3,0,1,2:T(8,128)(2,1)S(1)} %bitcast.245), channel_id=1, source_target_pairs={{0,8},{8,0},{1,9},{9,1},{2,10},{10,2},{3,11},{11,3},{4,12},{12,4},... | collective-permute-start | bytes 3145736 | tf_op jit(solution)/shard_map/ppermute | solution.py:44
  72.2 16.6 %collective-permute-start.8 = (bf16[2,2,2,128,512]{4,3,2,1,0:T(8,128)(2,1)S(1)}, bf16[2,2,2,128,512]{4,3,2,1,0:T(8,128)(2,1)S(1)}, u32[]{:S(2)}, u32[]{:S(2)}) collective-permute-start(bf16[2,2,2,128,512]{4,3,2,1,0:T(8,128)(2,1)S(1)} %slice_bitcast_fusion.6), channel_id=1, source_target_pairs={{0,8},{8,0},{1,9},{9,1},{2,10},{10,2},{3,11},{11,3},{4,12},{12,4},... | collective-permute-start | bytes 3145736 | tf_op jit(solution)/shard_map/ppermute | solution.py:44
  81.6 3.7 %copy-start.2 = (bf16[2,2,2,2,2,32,2048]{6,5,4,3,2,1,0:T(8,128)(2,1)}, bf16[2,2,2,2,2,32,2048]{6,5,4,3,2,1,0:T(8,128)(2,1)S(1)}, u32[]{:S(2)}) copy-start(bf16[2,2,2,2,2,32,2048]{6,5,4,3,2,1,0:T(8,128)(2,1)S(1)} %get-tuple-element.17) | copy-start | bytes 12582916
  81.6 9.9 %copy-start = (bf16[2,2,2,2,2,32,2048]{6,5,4,3,2,1,0:T(8,128)(2,1)}, bf16[2,2,2,2,2,32,2048]{6,5,4,3,2,1,0:T(8,128)(2,1)S(1)}, u32[]{:S(2)}) copy-start(bf16[2,2,2,2,2,32,2048]{6,5,4,3,2,1,0:T(8,128)(2,1)S(1)} %get-tuple-element.16) | copy-start | bytes 12582916
  83.3 36.3 %collective-permute-start = (bf16[2,2,2,2,32,2048]{5,4,3,2,1,0:T(8,128)(2,1)}, bf16[2,2,2,2,32,2048]{5,4,3,2,1,0:T(8,128)(2,1)}, u32[]{:S(2)}, u32[]{:S(2)}) collective-permute-start(bf16[2,2,2,2,32,2048]{5,4,3,2,1,0:T(8,128)(2,1)} %slice_bitcast_fusion.4), channel_id=1, source_target_pairs={{0,8},{8,0},{1,9},{9,1},{2,10},{10,2},{3,11},{11,3},{4,12},{12,4},... | collective-permute-start | bytes 6291464 | tf_op jit(solution)/shard_map/ppermute | solution.py:44
  85.3 16.5 %collective-permute-start.13 = (bf16[2,2,128,512]{3,2,0,1:T(8,128)(2,1)}, bf16[2,2,128,512]{3,2,0,1:T(8,128)(2,1)}, u32[]{:S(2)}, u32[]{:S(2)}) collective-permute-start(bf16[2,2,128,512]{3,2,0,1:T(8,128)(2,1)} %slice_bitcast_fusion.12), channel_id=1, source_target_pairs={{0,16},{16,0},{1,17},{17,1},{2,18},{18,2},{3,19},{19,3},{4,20},{20... | collective-permute-start | bytes 1572872 | tf_op jit(solution)/shard_map/ppermute | solution.py:44
  89.9 14.7 %collective-permute-start.9 = (bf16[2,2,128,512]{3,2,1,0:T(8,128)(2,1)}, bf16[2,2,128,512]{3,2,1,0:T(8,128)(2,1)}, u32[]{:S(2)}, u32[]{:S(2)}) collective-permute-start(bf16[2,2,128,512]{3,2,1,0:T(8,128)(2,1)} %slice_bitcast_fusion.14), channel_id=1, source_target_pairs={{0,32},{32,0},{64,96},{96,64},{1,33},{33,1},{65,97},{97,65},{2,34}... | collective-permute-start | bytes 1572872 | tf_op jit(solution)/shard_map/ppermute | solution.py:44
  93.1 30.5 %collective-permute-start.1 = (bf16[2,2,2,2,32,2048]{5,4,3,2,1,0:T(8,128)(2,1)}, bf16[2,2,2,2,32,2048]{5,4,3,2,1,0:T(8,128)(2,1)}, u32[]{:S(2)}, u32[]{:S(2)}) collective-permute-start(bf16[2,2,2,2,32,2048]{5,4,3,2,1,0:T(8,128)(2,1)} %slice_bitcast_fusion.2), channel_id=1, source_target_pairs={{0,8},{8,0},{1,9},{9,1},{2,10},{10,2},{3,11},{11,3},{4,12},{12,4},... | collective-permute-start | bytes 6291464 | tf_op jit(solution)/shard_map/ppermute | solution.py:44
  93.1 26.6 %copy-start.3 = (bf16[2,2,2,2,2,32,2048]{6,5,4,3,2,1,0:T(8,128)(2,1)S(1)}, bf16[2,2,2,2,2,32,2048]{6,5,4,3,2,1,0:T(8,128)(2,1)}, u32[]{:S(2)}) copy-start(bf16[2,2,2,2,2,32,2048]{6,5,4,3,2,1,0:T(8,128)(2,1)} %copy-done.2) | copy-start | bytes 12582916
  102.9 8.3 %collective-permute-start.14 = (bf16[2,128,512]{2,1,0:T(8,128)(2,1)S(1)}, bf16[2,128,512]{2,1,0:T(8,128)(2,1)S(1)}, u32[]{:S(2)}, u32[]{:S(2)}) collective-permute-start(bf16[2,128,512]{2,1,0:T(8,128)(2,1)S(1)} %slice_bitcast_fusion.20), channel_id=1, source_target_pairs={{0,32},{32,0},{64,96},{96,64},{1,33},{33,1},{65,97},{97,65},{2,34}... | collective-permute-start | bytes 786440 | tf_op jit(solution)/shard_map/ppermute | solution.py:44
  105.8 17.8 %copy-start.1 = (bf16[2,2,2,2,2,32,2048]{6,5,4,3,2,1,0:T(8,128)(2,1)S(1)}, bf16[2,2,2,2,2,32,2048]{6,5,4,3,2,1,0:T(8,128)(2,1)}, u32[]{:S(2)}) copy-start(bf16[2,2,2,2,2,32,2048]{6,5,4,3,2,1,0:T(8,128)(2,1)} %copy-done) | copy-start | bytes 12582916
  105.8 9.5 %collective-permute-start.10 = (bf16[2,128,512]{2,1,0:T(8,128)(2,1)S(1)}, bf16[2,128,512]{2,1,0:T(8,128)(2,1)S(1)}, u32[]{:S(2)}, u32[]{:S(2)}) collective-permute-start(bf16[2,128,512]{2,1,0:T(8,128)(2,1)S(1)} %slice_bitcast_fusion.22), channel_id=1, source_target_pairs={{0,16},{16,0},{1,17},{17,1},{2,18},{18,2},{3,19},{19,3},{4,20},{20... | collective-permute-start | bytes 786440 | tf_op jit(solution)/shard_map/ppermute | solution.py:44
  111.3 34.7 %collective-permute-start.15 = (bf16[128,512]{1,0:T(8,128)(2,1)S(1)}, bf16[128,512]{1,0:T(8,128)(2,1)}, u32[]{:S(2)}, u32[]{:S(2)}) collective-permute-start(bf16[128,512]{1,0:T(8,128)(2,1)S(1)} %slice_bitcast_fusion.28), channel_id=1, source_target_pairs={{0,64},{32,96},{64,0},{96,32},{1,65},{33,97},{65,1},{97,33},{2,66}... | collective-permute-start | bytes 393224 | tf_op jit(solution)/shard_map/ppermute | solution.py:44
  115.4 0.7 copy-start.8
  116.7 30.2 %collective-permute-start.11 = (bf16[128,512]{1,0:T(8,128)(2,1)}, bf16[128,512]{1,0:T(8,128)(2,1)}, u32[]{:S(2)}, u32[]{:S(2)}) collective-permute-start(bf16[128,512]{1,0:T(8,128)(2,1)} %slice_bitcast_fusion.30), channel_id=1, source_target_pairs={{0,64},{32,96},{64,0},{96,32},{1,65},{33,97},{65,1},{97,33},{2,66}... | collective-permute-start | bytes 393224 | tf_op jit(solution)/shard_map/ppermute | solution.py:44
  119.6 6.4 %copy-start.13 = (bf16[2,512,2048]{2,1,0:T(8,128)(2,1)S(1)}, bf16[2,512,2048]{2,1,0:T(8,128)(2,1)}, u32[]{:S(2)}) copy-start(bf16[2,512,2048]{2,1,0:T(8,128)(2,1)} %get-tuple-element.10) | copy-start | bytes 12582916
  123.6 2.8 %copy-start.6 = (bf16[2,512,2048]{2,1,0:T(8,128)(2,1)S(1)}, bf16[2,512,2048]{2,1,0:T(8,128)(2,1)}, u32[]{:S(2)}) copy-start(bf16[2,512,2048]{2,1,0:T(8,128)(2,1)} %param.10) | copy-start | bytes 12582916
  138.1 19.2 %all-to-all-start.3 = ((bf16[16,2,32,512]{3,2,1,0:T(8,128)(2,1)}), bf16[16,2,32,512]{3,2,1,0:T(8,128)(2,1)S(1)}, u32[]{:S(2)}, u32[]{:S(2)}) async-start(bf16[16,2,32,512]{3,2,1,0:T(8,128)(2,1)} %bitcast.238), calls=%async_computation.3 | async-start | bytes 2097152 | tf_op jit(solution)/shard_map/all_to_all | solution.py:156
  145.5 23.4 %collective-permute-start.2 = (bf16[2,2,2,32,2048]{4,3,2,1,0:T(8,128)(2,1)}, bf16[2,2,2,32,2048]{4,3,2,1,0:T(8,128)(2,1)}, u32[]{:S(2)}, u32[]{:S(2)}) collective-permute-start(bf16[2,2,2,32,2048]{4,3,2,1,0:T(8,128)(2,1)} %slice_bitcast_fusion.11), channel_id=1, source_target_pairs={{0,32},{32,0},{64,96},{96,64},{1,33},{33,1},{65,97},{97,65},{2,34}... | collective-permute-start | bytes 3145736 | tf_op jit(solution)/shard_map/ppermute | solution.py:44
  149.0 31.6 %collective-permute-start.5 = (bf16[2,2,2,32,2048]{4,3,2,1,0:T(8,128)(2,1)}, bf16[2,2,2,32,2048]{4,3,2,1,0:T(8,128)(2,1)}, u32[]{:S(2)}, u32[]{:S(2)}) collective-permute-start(bf16[2,2,2,32,2048]{4,3,2,1,0:T(8,128)(2,1)} %slice_bitcast_fusion.10), channel_id=1, source_target_pairs={{0,16},{16,0},{1,17},{17,1},{2,18},{18,2},{3,19},{19,3},{4,20},{20... | collective-permute-start | bytes 3145736 | tf_op jit(solution)/shard_map/ppermute | solution.py:44
  170.9 19.9 %collective-permute-start.3 = (bf16[2,2,32,2048]{3,2,1,0:T(8,128)(2,1)S(1)}, bf16[2,2,32,2048]{3,2,1,0:T(8,128)(2,1)S(1)}, u32[]{:S(2)}, u32[]{:S(2)}) collective-permute-start(bf16[2,2,32,2048]{3,2,1,0:T(8,128)(2,1)S(1)} %slice_bitcast_fusion.18), channel_id=1, source_target_pairs={{0,16},{16,0},{1,17},{17,1},{2,18},{18,2},{3,19},{19,3},{4,20},{20... | collective-permute-start | bytes 1572872 | tf_op jit(solution)/shard_map/ppermute | solution.py:44
  182.2 14.8 %collective-permute-start.6 = (bf16[2,2,32,2048]{3,2,1,0:T(8,128)(2,1)S(1)}, bf16[2,2,32,2048]{3,2,1,0:T(8,128)(2,1)S(1)}, u32[]{:S(2)}, u32[]{:S(2)}) collective-permute-start(bf16[2,2,32,2048]{3,2,1,0:T(8,128)(2,1)S(1)} %slice_bitcast_fusion.16), channel_id=1, source_target_pairs={{0,32},{32,0},{64,96},{96,64},{1,33},{33,1},{65,97},{97,65},{2,34}... | collective-permute-start | bytes 1572872 | tf_op jit(solution)/shard_map/ppermute | solution.py:44
  191.0 10.8 %collective-permute-start.4 = (bf16[2,32,2048]{2,1,0:T(8,128)(2,1)S(1)}, bf16[2,32,2048]{2,1,0:T(8,128)(2,1)S(1)}, u32[]{:S(2)}, u32[]{:S(2)}) collective-permute-start(bf16[2,32,2048]{2,1,0:T(8,128)(2,1)S(1)} %slice_bitcast_fusion.26), channel_id=1, source_target_pairs={{0,64},{32,96},{64,0},{96,32},{1,65},{33,97},{65,1},{97,33},{2,66}... | collective-permute-start | bytes 786440 | tf_op jit(solution)/shard_map/ppermute | solution.py:44
  197.3 8.4 %collective-permute-start.7 = (bf16[2,32,2048]{2,1,0:T(8,128)(2,1)S(1)}, bf16[2,32,2048]{2,1,0:T(8,128)(2,1)S(1)}, u32[]{:S(2)}, u32[]{:S(2)}) collective-permute-start(bf16[2,32,2048]{2,1,0:T(8,128)(2,1)S(1)} %slice_bitcast_fusion.24), channel_id=1, source_target_pairs={{0,64},{32,96},{64,0},{96,32},{1,65},{33,97},{65,1},{97,33},{2,66}... | collective-permute-start | bytes 786440 | tf_op jit(solution)/shard_map/ppermute | solution.py:44

commit v2 on v1

--- a/solution.py
+++ b/solution.py
@@ -136,7 +136,6 @@
     ).astype(jnp.bfloat16)
     gate_core = tree_reduce(gate_up_part[0], ORDER_A[:1], 1).astype(jnp.bfloat16)
     up_core = tree_reduce(gate_up_part[1], ORDER_B[:1], 1).astype(jnp.bfloat16)
-    gate_core, up_core, d_gate, d_up = lax.optimization_barrier((gate_core, up_core, d_gate, d_up))
     rest = ("dy1", "dy0", "dz")
     gate_grad = tree_reduce(gate_core, ORDER_A[1:], 1, rest)
     up_grad = tree_reduce(up_core, ORDER_B[1:], 1, rest)
@@ -153,9 +152,9 @@
     ).astype(jnp.bfloat16)
     d_mixed = d_mixed.reshape(blocks_here, block_total, piece, tok_count).transpose(1, 0, 2, 3)
 
-    d_features = lax.all_to_all(
-        d_mixed, "mp", split_axis=0, concat_axis=1, tiled=True
-    ).reshape(features.shape)
+    d_features = lax.all_to_all(d_mixed, "mp", split_axis=0, concat_axis=1, tiled=True).reshape(
+        features.shape
+    )
     return (outputs, d_features, gate_grad, up_grad, down_grad)
 
 

time: 208 us -> 211 us (1.014)
  waiting for transfers between devices: 62.3 us -> 71.6 us
  other arithmetic: 19.1 us -> 13.3 us
  starting transfers between devices: 44 us -> 40.7 us
  matrix products: 51.8 us -> 54.4 us
    all_to_all x1, waiting for transfers between devices: 4.2 us -> 12 us  [local(): lax.all_to_all(d_mixed, 'mp', split_axis=0, concat_axis=1, tiled=True)]
    squeeze x15, local copies, waits for them, and re-layouts: 9.97 us -> 5.57 us  [tree_reduce(): lax.index_in_dim(acc, 1, axis, keepdims=False)]
    dot_general x1, matrix products: 3.73 us -> 7.21 us  [local(): jnp.einsum('bth,bih->bit', d_gate, w_gate, preferred_element_type=jnp.flo...]
    ppermute x16, starting transfers between devices: 25.3 us -> 22 us  [tree_reduce(): lax.ppermute(lax.index_in_dim(acc, 1, axis, keepdims=False), name, perm=p...]
    convert_element_type x10, other arithmetic: 6.87 us -> 4.43 us  [tree_reduce(): acc = total.astype(jnp.bfloat16)]
    unnamed x47 -> x43, local copies, waits for them, and re-layouts: 9.1 us -> 10.4 us
  transfers between devices with their start and end apart: 20 -> 20, of which waited for: 12 -> 11; matrix products, arithmetic and copies ran while one was open for 36% -> 34% of each run, Pallas kernels for 0% -> 0%
where the time goes in v2:
time: 211 us
  waiting for transfers between devices  71.6 us (34%)
  matrix products  54.4 us (26%)
  starting transfers between devices  40.7 us (19%)
  local copies, waits for them, and re-layouts  29.4 us (14%)
  other arithmetic  13.3 us (6%)
    ppermute x16, waiting for transfers between devices, tree_reduce(): lax.ppermute(lax.index_in_dim(acc, 1, axis, keepdims=False), name, perm=p...  49.7 us
    ppermute x16, starting transfers between devices, tree_reduce(): lax.ppermute(lax.index_in_dim(acc, 1, axis, keepdims=False), name, perm=p...  22 us
    dot_general x1, matrix products, local(): jnp.einsum('sbkt,bhsk->bth', cot_blocks, down_view, preferred_element_typ...  14.1 us
    all_to_all x1, waiting for transfers between devices, local(): lax.all_to_all(d_mixed, 'mp', split_axis=0, concat_axis=1, tiled=True)  12 us
    unnamed x43, local copies, waits for them, and re-layouts  10.4 us
    all_to_all x1, waiting for transfers between devices, local(): lax.all_to_all(features.reshape(local_shape), 'mp', split_axis=1, concat_...  8.57 us
    dot_general x1, matrix products, local(): jnp.einsum('bth,bih->bit', d_gate, w_gate, preferred_element_type=jnp.flo...  7.21 us
    dot_general x1, matrix products, local(): jnp.einsum('bij,bit->bjt', onehot, d_mixed_p, preferred_element_type=jnp....  6.97 us
  transfers between devices with their start and end apart: 20, of which 11 were waited for; matrix products, arithmetic and copies ran while one was open for 34% of the time, Pallas kernels for 0%

profile of v2, /device:TPU:0, one launch (start us, length us, event | category | flops | bytes accessed | tf_op | source)
XLA Modules:
  0.0 210.6 jit_solution(1226144286077229157)
XLA Ops:
  0.6 2.4 %copy.78 = bf16[2,16,32,512]{3,2,0,1:T(8,128)(2,1)} copy(bf16[2,16,32,512]{3,2,1,0:T(8,128)(2,1)} %bitcast.243) | data formatting | bytes 2097152 | tf_op jit(solution)/shard_map/reshape | solution.py:70
  3.0 5.8 %all-to-all-start = ((bf16[2,16,32,512]{3,2,0,1:T(8,128)(2,1)}), bf16[2,16,32,512]{3,2,0,1:T(8,128)(2,1)S(1)}, u32[]{:S(2)}, u32[]{:S(2)}) async-start(bf16[2,16,32,512]{3,2,0,1:T(8,128)(2,1)} %copy.78), calls=%async_computation | async-start | bytes 2097152 | tf_op jit(solution)/shard_map/all_to_all | solution.py:69
  9.9 6.3 %copy.83 = bf16[2,2048,512]{1,2,0:T(8,128)(2,1)} copy(bf16[2,2048,512]{2,1,0:T(8,128)(2,1)} %param.11) | data formatting | bytes 8388608 | tf_op args[5]
  16.1 8.6 %all-to-all-done = bf16[2,16,32,512]{3,2,0,1:T(8,128)(2,1)S(1)} async-done(((bf16[2,16,32,512]{3,2,0,1:T(8,128)(2,1)}), bf16[2,16,32,512]{3,2,0,1:T(8,128)(2,1)S(1)}, u32[]{:S(2)}, u32[]{:S(2)}) %all-to-all-start) | async-done | bytes 1048608 | tf_op jit(solution)/shard_map/all_to_all | solution.py:69
  24.7 3.6 %all-to-all-start.2 = ((bf16[2,16,32,512]{3,2,0,1:T(8,128)(2,1)}), bf16[2,16,32,512]{3,2,0,1:T(8,128)(2,1)S(1)}, u32[]{:S(2)}, u32[]{:S(2)}) async-start(bf16[2,16,32,512]{3,2,0,1:T(8,128)(2,1)} %copy.86), calls=%async_computation.2 | async-start | bytes 2097152 | tf_op jit(solution)/shard_map/all_to_all | solution.py:72
  29.1 1.3 copy-done.7
  30.5 5.7 %fusion.31 = f32[2,512,2048]{2,1,0:T(8,128)} fusion(bf16[2,512,512]{2,1,0:T(8,128)(2,1)S(1)} %fusion.14, bf16[2,512,2048]{2,1,0:T(8,128)(2,1)S(1)} %copy-done.7), kind=kOutput, calls=%fused_computation.112 | convolution fusion | flops 2147483648 | bytes 13631488 | tf_op jit(solution)/shard_map/bit,bih->bth/dot_general | solution.py:83
  36.1 5.6 %fusion.32 = f32[2,512,2048]{2,1,0:T(8,128)} fusion(bf16[2,512,512]{2,1,0:T(8,128)(2,1)S(1)} %fusion.14, bf16[2,512,2048]{2,1,0:T(8,128)(2,1)S(1)} %copy-done.8), kind=kOutput, calls=%fused_computation.113 | convolution fusion | flops 2147483648 | bytes 13631488 | tf_op jit(solution)/shard_map/bit,bih->bth/dot_general | solution.py:87
  41.8 1.4 all-to-all-done.2
  43.3 14.1 %multiply_convert_fusion.2 = (bf16[2,512,2048]{2,1,0:T(8,128)(2,1)}, bf16[2,512,2048]{2,1,0:T(8,128)(2,1)}, bf16[2,512,2048]{2,1,0:T(8,128)(2,1)S(1)}) fusion(f32[2,512,2048]{2,1,0:T(8,128)} %fusion.31, f32[2,512,2048]{2,1,0:T(8,128)} %fusion.32, bf16[16,2,32,512]{3,2,0,1:T(8,128)(2,1)S(1)} %bitcast.248, bf16[2,2048,16,32]{1,3,2,0:T(8,128)(2,1)} %bitcast.238), kind=kOutput, calls=%fused_computation.7 | convolution fusion | flops 2185232384 | bytes 34603008 | tf_op jit(solution)/shard_map/sbkt,bhsk->bth/dot_general | solution.py:121
  57.4 2.4 %fusion.33 = f32[2,512,512]{1,2,0:S(1)} fusion(bf16[2,512,2048]{2,1,0:T(8,128)(2,1)S(1)} %get-tuple-element.7, bf16[2,2048,512]{2,1,0:T(8,128)(2,1)S(1)} %copy-done.6), kind=kOutput, calls=%fused_computation.114 | convolution fusion | flops 2147483648 | bytes 10485760
  61.2 4.4 %all-to-all-start.1 = ((bf16[16,2,32,512]{3,2,1,0:T(8,128)(2,1)}), bf16[16,2,32,512]{3,2,1,0:T(8,128)(2,1)}, u32[]{:S(2)}, u32[]{:S(2)}) async-start(bf16[16,2,32,512]{3,2,1,0:T(8,128)(2,1)} %copy.84), calls=%async_computation.1 | async-start | bytes 2097152 | tf_op jit(solution)/shard_map/all_to_all | solution.py:116
  65.6 7.2 %fusion.34 = f32[2,512,512]{2,1,0:T(8,128)} fusion(bf16[2,512,2048]{2,1,0:T(8,128)(2,1)} %get-tuple-element.6, bf16[2,512,2048]{2,1,0:T(8,128)(2,1)} %param.9), kind=kOutput, calls=%fused_computation.115 | convolution fusion | flops 2147483648 | bytes 10485760 | tf_op jit(solution)/shard_map/bth,bih->bit/dot_general | solution.py:145
  72.8 7.0 %fusion.15 = bf16[2,512,512]{2,1,0:T(8,128)(2,1)S(1)} fusion(s32[2,512]{1,0:T(2,128)S(1)} %copy-done.10, f32[2,512,512]{2,1,0:T(8,128)} %fusion.34, bf16[2,512,2048]{2,1,0:T(8,128)(2,1)} %get-tuple-element.5, bf16[2,512,2048]{2,1,0:T(8,128)(2,1)} %param.10), kind=kOutput, calls=%fused_computation.40 | convolution fusion | flops 2686976000 | bytes 11538432 | tf_op jit(solution)/shard_map/bij,bit->bjt/dot_general | solution.py:150
  79.8 1.1 copy.139
  80.9 5.3 %multiply_convert_fusion.1 = bf16[2,2048,512]{2,1,0:T(8,128)(2,1)S(1)} fusion(bf16[2,512,2048]{2,1,0:T(8,128)(2,1)} %copy-done.12, bf16[2,512,512]{2,1,0:T(8,128)(2,1)S(1)} %bitcast.249), kind=kOutput, calls=%fused_computation.6 | convolution fusion | flops 2151677952 | bytes 9437184 | tf_op jit(solution)/shard_map/bth,bjt->bhj/dot_general | solution.py:100
  87.3 1.1 slice_bitcast_fusion.6
  90.0 1.4 copy-done.11
  91.3 6.4 %fusion = bf16[2,2,2,2,2,2,32,2048]{7,6,5,4,3,2,0,1:T(8,128)(2,1)S(1)} fusion(bf16[2,2,2,2,2,32,512,1]{6,5,4,3,2,1,7,0:T(8,128)(2,1)S(1)} %fusion.16, bf16[1,2,512,2048]{3,2,1,0:T(8,128)(2,1)S(1)} %bitcast.252, bf16[1,2,512,2048]{3,2,1,0:T(8,128)(2,1)} %bitcast.253), kind=kOutput, calls=%fused_computation.1 | convolution fusion | flops 4307550208 | bytes 17825792 | tf_op jit(solution)/shard_map/bwyzcrt,gbth->gbwyzcrh/dot_general | solution.py:132
  97.8 2.3 %slice_bitcast_fusion = (bf16[2,2,2,2,2,32,2048]{6,5,4,3,2,1,0:T(8,128)(2,1)}, bf16[2,2,2,2,2,32,2048]{6,5,4,3,2,1,0:T(8,128)(2,1)S(1)}) fusion(bf16[2,2,2,2,2,2,32,2048]{7,6,5,4,3,2,0,1:T(8,128)(2,1)S(1)} %fusion), kind=kLoop, calls=%fused_computation.12 | loop fusion | bytes 16777216 | tf_op jit(solution)/shard_map/squeeze | solution.py:138
  100.1 1.8 slice_bitcast_fusion.4
  103.0 3.6 %collective-permute-start.13 = (bf16[2,2,128,512]{3,2,0,1:T(8,128)(2,1)}, bf16[2,2,128,512]{3,2,0,1:T(8,128)(2,1)}, u32[]{:S(2)}, u32[]{:S(2)}) collective-permute-start(bf16[2,2,128,512]{3,2,0,1:T(8,128)(2,1)} %slice_bitcast_fusion.12), channel_id=1, source_target_pairs={{0,16},{16,0},{1,17},{17,1},{2,18},{18,2},{3,19},{19,3},{4,20},{20... | collective-permute-start | bytes 1572872 | tf_op jit(solution)/shard_map/ppermute | solution.py:44
  106.6 4.9 %all-to-all-start.3 = ((bf16[16,2,32,512]{3,2,1,0:T(8,128)(2,1)}), bf16[16,2,32,512]{3,2,1,0:T(8,128)(2,1)}, u32[]{:S(2)}, u32[]{:S(2)}) async-start(bf16[16,2,32,512]{3,2,1,0:T(8,128)(2,1)} %bitcast.240), calls=%async_computation.3 | async-start | bytes 2097152 | tf_op jit(solution)/shard_map/all_to_all | solution.py:155
  111.5 1.7 fusion.9
  114.2 1.7 collective-permute-start.9
  115.9 1.4 slice_bitcast_fusion.2
  117.3 2.4 %copy.85 = bf16[2,8,2,32,512]{4,3,2,1,0:T(8,128)(2,1)} copy(bf16[2,8,2,32,512]{4,3,2,0,1:T(8,128)(2,1)} %bitcast.11) | data formatting | bytes 2097152 | tf_op jit(solution)/shard_map/all_to_all | solution.py:116
  119.7 12.0 %all-to-all-done.3 = bf16[16,2,32,512]{3,2,1,0:T(8,128)(2,1)} async-done(((bf16[16,2,32,512]{3,2,1,0:T(8,128)(2,1)}), bf16[16,2,32,512]{3,2,1,0:T(8,128)(2,1)}, u32[]{:S(2)}, u32[]{:S(2)}) %all-to-all-start.3) | async-done | bytes 1048608 | tf_op jit(solution)/shard_map/all_to_all | solution.py:155
  131.7 2.5 %copy.90 = bf16[2,8,2,32,512]{4,3,2,1,0:T(8,128)(2,1)} copy(bf16[2,8,2,32,512]{4,3,2,0,1:T(8,128)(2,1)} %bitcast.23) | data formatting | bytes 2097152 | tf_op jit(solution)/shard_map/all_to_all | solution.py:155
  134.1 1.2 fusion.18
  135.4 1.7 collective-permute-start.14
  137.2 1.2 collective-permute-start.10
  138.4 4.9 %collective-permute-done.14 = bf16[2,128,512]{2,1,0:T(8,128)(2,1)S(1)} collective-permute-done((bf16[2,128,512]{2,1,0:T(8,128)(2,1)S(1)}, bf16[2,128,512]{2,1,0:T(8,128)(2,1)S(1)}, u32[]{:S(2)}, u32[]{:S(2)}) %collective-permute-start.14) | collective-permute-done | bytes 262176 | tf_op jit(solution)/shard_map/ppermute | solution.py:44
  143.4 3.3 %collective-permute-start.15 = (bf16[128,512]{1,0:T(8,128)(2,1)S(1)}, bf16[128,512]{1,0:T(8,128)(2,1)S(1)}, u32[]{:S(2)}, u32[]{:S(2)}) collective-permute-start(bf16[128,512]{1,0:T(8,128)(2,1)S(1)} %slice_bitcast_fusion.28), channel_id=1, source_target_pairs={{0,64},{32,96},{64,0},{96,32},{1,65},{33,97},{65,1},{97,33},{2,66}... | collective-permute-start | bytes 393224 | tf_op jit(solution)/shard_map/ppermute | solution.py:44
  146.7 2.7 %collective-permute-start.11 = (bf16[128,512]{1,0:T(8,128)(2,1)S(1)}, bf16[128,512]{1,0:T(8,128)(2,1)S(1)}, u32[]{:S(2)}, u32[]{:S(2)}) collective-permute-start(bf16[128,512]{1,0:T(8,128)(2,1)S(1)} %slice_bitcast_fusion.30), channel_id=1, source_target_pairs={{0,64},{32,96},{64,0},{96,32},{1,65},{33,97},{65,1},{97,33},{2,66}... | collective-permute-start | bytes 393224 | tf_op jit(solution)/shard_map/ppermute | solution.py:44
  150.5 2.8 %collective-permute-done.11 = bf16[128,512]{1,0:T(8,128)(2,1)S(1)} collective-permute-done((bf16[128,512]{1,0:T(8,128)(2,1)S(1)}, bf16[128,512]{1,0:T(8,128)(2,1)S(1)}, u32[]{:S(2)}, u32[]{:S(2)}) %collective-permute-start.11) | collective-permute-done | bytes 131104 | tf_op jit(solution)/shard_map/ppermute | solution.py:44
  153.4 2.5 %fusion.7 = bf16[2,2,2,2,32,2048]{5,4,3,2,1,0:T(8,128)(2,1)S(1)} fusion(bf16[2,2,2,2,32,2048]{5,4,3,2,1,0:T(8,128)(2,1)} %collective-permute-done, bf16[2,2,2,2,2,32,2048]{6,5,4,3,2,1,0:T(8,128)(2,1)S(1)} %copy-done.3), kind=kLoop, calls=%fused_computation.17 | loop fusion | flops 4194304 | bytes 6291456 | tf_op jit(solution)/shard_map/convert_element_type | solution.py:137
  156.0 1.1 collective-permute-start.1
  157.1 2.4 %fusion.6 = bf16[2,2,2,2,32,2048]{5,4,3,2,1,0:T(8,128)(2,1)S(1)} fusion(bf16[2,2,2,2,32,2048]{5,4,3,2,1,0:T(8,128)(2,1)} %collective-permute-done.4, bf16[2,2,2,2,2,32,2048]{6,5,4,3,2,1,0:T(8,128)(2,1)S(1)} %copy-done.1), kind=kLoop, calls=%fused_computation.15 | loop fusion | flops 4194304 | bytes 6291456 | tf_op jit(solution)/shard_map/convert_element_type | solution.py:138
  159.6 1.2 collective-permute-start.5
  161.6 17.5 %collective-permute-done.1 = bf16[2,2,2,32,2048]{4,3,2,1,0:T(8,128)(2,1)S(1)} collective-permute-done((bf16[2,2,2,32,2048]{4,3,2,1,0:T(8,128)(2,1)S(1)}, bf16[2,2,2,32,2048]{4,3,2,1,0:T(8,128)(2,1)S(1)}, u32[]{:S(2)}, u32[]{:S(2)}) %collective-permute-start.1) | collective-permute-done | bytes 1048608 | tf_op jit(solution)/shard_map/ppermute | solution.py:44
  179.6 1.2 collective-permute-start.2
  180.8 6.4 %collective-permute-done.5 = bf16[2,2,2,32,2048]{4,3,2,1,0:T(8,128)(2,1)S(1)} collective-permute-done((bf16[2,2,2,32,2048]{4,3,2,1,0:T(8,128)(2,1)S(1)}, bf16[2,2,2,32,2048]{4,3,2,1,0:T(8,128)(2,1)S(1)}, u32[]{:S(2)}, u32[]{:S(2)}) %collective-permute-start.5) | collective-permute-done | bytes 1048608 | tf_op jit(solution)/shard_map/ppermute | solution.py:44
  187.7 8.2 %collective-permute-done.2 = bf16[2,2,32,2048]{3,2,1,0:T(8,128)(2,1)S(1)} collective-permute-done((bf16[2,2,32,2048]{3,2,1,0:T(8,128)(2,1)S(1)}, bf16[2,2,32,2048]{3,2,1,0:T(8,128)(2,1)S(1)}, u32[]{:S(2)}, u32[]{:S(2)}) %collective-permute-start.2) | collective-permute-done | bytes 524320 | tf_op jit(solution)/shard_map/ppermute | solution.py:44
  196.0 2.5 %collective-permute-start.3 = (bf16[2,32,2048]{2,1,0:T(8,128)(2,1)S(1)}, bf16[2,32,2048]{2,1,0:T(8,128)(2,1)S(1)}, u32[]{:S(2)}, u32[]{:S(2)}) collective-permute-start(bf16[2,32,2048]{2,1,0:T(8,128)(2,1)S(1)} %slice_bitcast_fusion.26), channel_id=1, source_target_pairs={{0,64},{32,96},{64,0},{96,32},{1,65},{33,97},{65,1},{97,33},{2,66}... | collective-permute-start | bytes 786440 | tf_op jit(solution)/shard_map/ppermute | solution.py:44
  198.7 1.2 collective-permute-start.7
  199.9 6.9 %collective-permute-done.3 = bf16[2,32,2048]{2,1,0:T(8,128)(2,1)S(1)} collective-permute-done((bf16[2,32,2048]{2,1,0:T(8,128)(2,1)S(1)}, bf16[2,32,2048]{2,1,0:T(8,128)(2,1)S(1)}, u32[]{:S(2)}, u32[]{:S(2)}) %collective-permute-start.3) | collective-permute-done | bytes 262176 | tf_op jit(solution)/shard_map/ppermute | solution.py:44
  207.7 2.1 collective-permute-done.7
  (93 shorter events, 13.5 us)
Async XLA Ops:
  0.6 8.2 %copy-start.9 = (bf16[1024,512]{1,0:T(8,128)(2,1)S(1)}, bf16[1024,512]{1,0:T(8,128)(2,1)}, u32[]{:S(2)}) copy-start(bf16[1024,512]{1,0:T(8,128)(2,1)} %param.7) | copy-start | bytes 3145732
  3.0 21.7 %all-to-all-start = ((bf16[2,16,32,512]{3,2,0,1:T(8,128)(2,1)}), bf16[2,16,32,512]{3,2,0,1:T(8,128)(2,1)S(1)}, u32[]{:S(2)}, u32[]{:S(2)}) async-start(bf16[2,16,32,512]{3,2,0,1:T(8,128)(2,1)} %copy.78), calls=%async_computation | async-start | bytes 2097152 | tf_op jit(solution)/shard_map/all_to_all | solution.py:69
  16.1 12.2 %copy-start.10 = (s32[2,512]{1,0:T(2,128)S(1)}, s32[2,512]{1,0:T(2,128)}, u32[]{:S(2)}) copy-start(s32[2,512]{1,0:T(2,128)} %param.8) | copy-start | bytes 12292
  24.7 18.5 %all-to-all-start.2 = ((bf16[2,16,32,512]{3,2,0,1:T(8,128)(2,1)}), bf16[2,16,32,512]{3,2,0,1:T(8,128)(2,1)S(1)}, u32[]{:S(2)}, u32[]{:S(2)}) async-start(bf16[2,16,32,512]{3,2,0,1:T(8,128)(2,1)} %copy.86), calls=%async_computation.2 | async-start | bytes 2097152 | tf_op jit(solution)/shard_map/all_to_all | solution.py:72
  28.3 2.2 %copy-start.7 = (bf16[2,512,2048]{2,1,0:T(8,128)(2,1)S(1)}, bf16[2,512,2048]{2,1,0:T(8,128)(2,1)}, u32[]{:S(2)}) copy-start(bf16[2,512,2048]{2,1,0:T(8,128)(2,1)} %param.9) | copy-start | bytes 12582916
  30.5 5.7 %copy-start.8 = (bf16[2,512,2048]{2,1,0:T(8,128)(2,1)S(1)}, bf16[2,512,2048]{2,1,0:T(8,128)(2,1)}, u32[]{:S(2)}) copy-start(bf16[2,512,2048]{2,1,0:T(8,128)(2,1)} %param.10) | copy-start | bytes 12582916
  43.3 14.2 %copy-start.6 = (bf16[2,2048,512]{2,1,0:T(8,128)(2,1)S(1)}, bf16[2,2048,512]{2,1,0:T(8,128)(2,1)}, u32[]{:S(2)}) copy-start(bf16[2,2048,512]{2,1,0:T(8,128)(2,1)} %param.11) | copy-start | bytes 12582916
  57.4 2.4 %copy-start.12 = (bf16[2,512,2048]{2,1,0:T(8,128)(2,1)}, bf16[2,512,2048]{2,1,0:T(8,128)(2,1)S(1)}, u32[]{:S(2)}) copy-start(bf16[2,512,2048]{2,1,0:T(8,128)(2,1)S(1)} %get-tuple-element.7) | copy-start | bytes 12582916
  61.2 45.4 %all-to-all-start.1 = ((bf16[16,2,32,512]{3,2,1,0:T(8,128)(2,1)}), bf16[16,2,32,512]{3,2,1,0:T(8,128)(2,1)}, u32[]{:S(2)}, u32[]{:S(2)}) async-start(bf16[16,2,32,512]{3,2,1,0:T(8,128)(2,1)} %copy.84), calls=%async_computation.1 | async-start | bytes 2097152 | tf_op jit(solution)/shard_map/all_to_all | solution.py:116
  87.2 14.7 %collective-permute-start.12 = (bf16[2,2,2,128,512]{4,3,0,1,2:T(8,128)(2,1)S(1)}, bf16[2,2,2,128,512]{4,3,0,1,2:T(8,128)(2,1)S(1)}, u32[]{:S(2)}, u32[]{:S(2)}) collective-permute-start(bf16[2,2,2,128,512]{4,3,0,1,2:T(8,128)(2,1)S(1)} %bitcast.247), channel_id=1, source_target_pairs={{0,8},{8,0},{1,9},{9,1},{2,10},{10,2},{3,11},{11,3},{4,12},{12,4},... | collective-permute-start | bytes 3145736 | tf_op jit(solution)/shard_map/ppermute | solution.py:44
  88.4 23.2 %collective-permute-start.8 = (bf16[2,2,2,128,512]{4,3,2,1,0:T(8,128)(2,1)}, bf16[2,2,2,128,512]{4,3,2,1,0:T(8,128)(2,1)}, u32[]{:S(2)}, u32[]{:S(2)}) collective-permute-start(bf16[2,2,2,128,512]{4,3,2,1,0:T(8,128)(2,1)} %slice_bitcast_fusion.6), channel_id=1, source_target_pairs={{0,8},{8,0},{1,9},{9,1},{2,10},{10,2},{3,11},{11,3},{4,12},{12,4},... | collective-permute-start | bytes 3145736 | tf_op jit(solution)/shard_map/ppermute | solution.py:44
  89.1 2.2 %copy-start.11 = (bf16[2,512,2048]{2,1,0:T(8,128)(2,1)S(1)}, bf16[2,512,2048]{2,1,0:T(8,128)(2,1)}, u32[]{:S(2)}) copy-start(bf16[2,512,2048]{2,1,0:T(8,128)(2,1)} %get-tuple-element.5) | copy-start | bytes 12582916
  100.1 3.0 %copy-start.2 = (bf16[2,2,2,2,2,32,2048]{6,5,4,3,2,1,0:T(8,128)(2,1)}, bf16[2,2,2,2,2,32,2048]{6,5,4,3,2,1,0:T(8,128)(2,1)S(1)}, u32[]{:S(2)}) copy-start(bf16[2,2,2,2,2,32,2048]{6,5,4,3,2,1,0:T(8,128)(2,1)S(1)} %get-tuple-element.9) | copy-start | bytes 12582916
  101.9 51.5 %collective-permute-start = (bf16[2,2,2,2,32,2048]{5,4,3,2,1,0:T(8,128)(2,1)}, bf16[2,2,2,2,32,2048]{5,4,3,2,1,0:T(8,128)(2,1)}, u32[]{:S(2)}, u32[]{:S(2)}) collective-permute-start(bf16[2,2,2,2,32,2048]{5,4,3,2,1,0:T(8,128)(2,1)} %slice_bitcast_fusion.4), channel_id=1, source_target_pairs={{0,8},{8,0},{1,9},{9,1},{2,10},{10,2},{3,11},{11,3},{4,12},{12,4},... | collective-permute-start | bytes 6291464 | tf_op jit(solution)/shard_map/ppermute | solution.py:44
  103.0 31.1 %collective-permute-start.13 = (bf16[2,2,128,512]{3,2,0,1:T(8,128)(2,1)}, bf16[2,2,128,512]{3,2,0,1:T(8,128)(2,1)}, u32[]{:S(2)}, u32[]{:S(2)}) collective-permute-start(bf16[2,2,128,512]{3,2,0,1:T(8,128)(2,1)} %slice_bitcast_fusion.12), channel_id=1, source_target_pairs={{0,16},{16,0},{1,17},{17,1},{2,18},{18,2},{3,19},{19,3},{4,20},{20... | collective-permute-start | bytes 1572872 | tf_op jit(solution)/shard_map/ppermute | solution.py:44
  106.6 25.1 %all-to-all-start.3 = ((bf16[16,2,32,512]{3,2,1,0:T(8,128)(2,1)}), bf16[16,2,32,512]{3,2,1,0:T(8,128)(2,1)}, u32[]{:S(2)}, u32[]{:S(2)}) async-start(bf16[16,2,32,512]{3,2,1,0:T(8,128)(2,1)} %bitcast.240), calls=%async_computation.3 | async-start | bytes 2097152 | tf_op jit(solution)/shard_map/all_to_all | solution.py:155
  111.5 4.4 %copy-start = (bf16[2,2,2,2,2,32,2048]{6,5,4,3,2,1,0:T(8,128)(2,1)S(1)}, bf16[2,2,2,2,2,32,2048]{6,5,4,3,2,1,0:T(8,128)(2,1)}, u32[]{:S(2)}) copy-start(bf16[2,2,2,2,2,32,2048]{6,5,4,3,2,1,0:T(8,128)(2,1)} %get-tuple-element.8) | copy-start | bytes 12582916
  113.2 1.0 copy-start.4
  114.2 22.8 %collective-permute-start.9 = (bf16[2,2,128,512]{3,2,1,0:T(8,128)(2,1)S(1)}, bf16[2,2,128,512]{3,2,1,0:T(8,128)(2,1)S(1)}, u32[]{:S(2)}, u32[]{:S(2)}) collective-permute-start(bf16[2,2,128,512]{3,2,1,0:T(8,128)(2,1)S(1)} %slice_bitcast_fusion.14), channel_id=1, source_target_pairs={{0,32},{32,0},{64,96},{96,64},{1,33},{33,1},{65,97},{97,65},{2,34}... | collective-permute-start | bytes 1572872 | tf_op jit(solution)/shard_map/ppermute | solution.py:44
  117.3 19.7 %copy-start.5 = (bf16[2,2,2,128,512]{4,3,2,1,0:T(8,128)(2,1)S(1)}, bf16[2,2,2,128,512]{4,3,2,1,0:T(8,128)(2,1)}, u32[]{:S(2)}) copy-start(bf16[2,2,2,128,512]{4,3,2,1,0:T(8,128)(2,1)} %copy-done.4) | copy-start | bytes 3145732
  117.3 39.8 %collective-permute-start.4 = (bf16[2,2,2,2,32,2048]{5,4,3,2,1,0:T(8,128)(2,1)}, bf16[2,2,2,2,32,2048]{5,4,3,2,1,0:T(8,128)(2,1)}, u32[]{:S(2)}, u32[]{:S(2)}) collective-permute-start(bf16[2,2,2,2,32,2048]{5,4,3,2,1,0:T(8,128)(2,1)} %slice_bitcast_fusion.2), channel_id=1, source_target_pairs={{0,8},{8,0},{1,9},{9,1},{2,10},{10,2},{3,11},{11,3},{4,12},{12,4},... | collective-permute-start | bytes 6291464 | tf_op jit(solution)/shard_map/ppermute | solution.py:44
  131.7 21.7 %copy-start.3 = (bf16[2,2,2,2,2,32,2048]{6,5,4,3,2,1,0:T(8,128)(2,1)S(1)}, bf16[2,2,2,2,2,32,2048]{6,5,4,3,2,1,0:T(8,128)(2,1)}, u32[]{:S(2)}) copy-start(bf16[2,2,2,2,2,32,2048]{6,5,4,3,2,1,0:T(8,128)(2,1)} %copy-done.2) | copy-start | bytes 12582916
  135.4 7.9 %collective-permute-start.14 = (bf16[2,128,512]{2,1,0:T(8,128)(2,1)S(1)}, bf16[2,128,512]{2,1,0:T(8,128)(2,1)S(1)}, u32[]{:S(2)}, u32[]{:S(2)}) collective-permute-start(bf16[2,128,512]{2,1,0:T(8,128)(2,1)S(1)} %slice_bitcast_fusion.20), channel_id=1, source_target_pairs={{0,32},{32,0},{64,96},{96,64},{1,33},{33,1},{65,97},{97,65},{2,34}... | collective-permute-start | bytes 786440 | tf_op jit(solution)/shard_map/ppermute | solution.py:44
  137.2 9.5 %collective-permute-start.10 = (bf16[2,128,512]{2,1,0:T(8,128)(2,1)S(1)}, bf16[2,128,512]{2,1,0:T(8,128)(2,1)S(1)}, u32[]{:S(2)}, u32[]{:S(2)}) collective-permute-start(bf16[2,128,512]{2,1,0:T(8,128)(2,1)S(1)} %slice_bitcast_fusion.22), channel_id=1, source_target_pairs={{0,16},{16,0},{1,17},{17,1},{2,18},{18,2},{3,19},{19,3},{4,20},{20... | collective-permute-start | bytes 786440 | tf_op jit(solution)/shard_map/ppermute | solution.py:44
  143.4 7.1 %collective-permute-start.15 = (bf16[128,512]{1,0:T(8,128)(2,1)S(1)}, bf16[128,512]{1,0:T(8,128)(2,1)S(1)}, u32[]{:S(2)}, u32[]{:S(2)}) collective-permute-start(bf16[128,512]{1,0:T(8,128)(2,1)S(1)} %slice_bitcast_fusion.28), channel_id=1, source_target_pairs={{0,64},{32,96},{64,0},{96,32},{1,65},{33,97},{65,1},{97,33},{2,66}... | collective-permute-start | bytes 393224 | tf_op jit(solution)/shard_map/ppermute | solution.py:44
  146.7 6.6 %collective-permute-start.11 = (bf16[128,512]{1,0:T(8,128)(2,1)S(1)}, bf16[128,512]{1,0:T(8,128)(2,1)S(1)}, u32[]{:S(2)}, u32[]{:S(2)}) collective-permute-start(bf16[128,512]{1,0:T(8,128)(2,1)S(1)} %slice_bitcast_fusion.30), channel_id=1, source_target_pairs={{0,64},{32,96},{64,0},{96,32},{1,65},{33,97},{65,1},{97,33},{2,66}... | collective-permute-start | bytes 393224 | tf_op jit(solution)/shard_map/ppermute | solution.py:44
  153.3 3.8 %copy-start.1 = (bf16[2,2,2,2,2,32,2048]{6,5,4,3,2,1,0:T(8,128)(2,1)S(1)}, bf16[2,2,2,2,2,32,2048]{6,5,4,3,2,1,0:T(8,128)(2,1)}, u32[]{:S(2)}) copy-start(bf16[2,2,2,2,2,32,2048]{6,5,4,3,2,1,0:T(8,128)(2,1)} %get-tuple-element.8) | copy-start | bytes 12582916
  156.0 23.1 %collective-permute-start.1 = (bf16[2,2,2,32,2048]{4,3,2,1,0:T(8,128)(2,1)S(1)}, bf16[2,2,2,32,2048]{4,3,2,1,0:T(8,128)(2,1)S(1)}, u32[]{:S(2)}, u32[]{:S(2)}) collective-permute-start(bf16[2,2,2,32,2048]{4,3,2,1,0:T(8,128)(2,1)S(1)} %slice_bitcast_fusion.10), channel_id=1, source_target_pairs={{0,32},{32,0},{64,96},{96,64},{1,33},{33,1},{65,97},{97,65},{2,34}... | collective-permute-start | bytes 3145736 | tf_op jit(solution)/shard_map/ppermute | solution.py:44
  159.6 27.6 %collective-permute-start.5 = (bf16[2,2,2,32,2048]{4,3,2,1,0:T(8,128)(2,1)S(1)}, bf16[2,2,2,32,2048]{4,3,2,1,0:T(8,128)(2,1)S(1)}, u32[]{:S(2)}, u32[]{:S(2)}) collective-permute-start(bf16[2,2,2,32,2048]{4,3,2,1,0:T(8,128)(2,1)S(1)} %slice_bitcast_fusion.8), channel_id=1, source_target_pairs={{0,16},{16,0},{1,17},{17,1},{2,18},{18,2},{3,19},{19,3},{4,20},{20... | collective-permute-start | bytes 3145736 | tf_op jit(solution)/shard_map/ppermute | solution.py:44
  179.6 16.3 %collective-permute-start.2 = (bf16[2,2,32,2048]{3,2,1,0:T(8,128)(2,1)S(1)}, bf16[2,2,32,2048]{3,2,1,0:T(8,128)(2,1)S(1)}, u32[]{:S(2)}, u32[]{:S(2)}) collective-permute-start(bf16[2,2,32,2048]{3,2,1,0:T(8,128)(2,1)S(1)} %slice_bitcast_fusion.18), channel_id=1, source_target_pairs={{0,16},{16,0},{1,17},{17,1},{2,18},{18,2},{3,19},{19,3},{4,20},{20... | collective-permute-start | bytes 1572872 | tf_op jit(solution)/shard_map/ppermute | solution.py:44
  187.6 10.9 %collective-permute-start.6 = (bf16[2,2,32,2048]{3,2,1,0:T(8,128)(2,1)S(1)}, bf16[2,2,32,2048]{3,2,1,0:T(8,128)(2,1)S(1)}, u32[]{:S(2)}, u32[]{:S(2)}) collective-permute-start(bf16[2,2,32,2048]{3,2,1,0:T(8,128)(2,1)S(1)} %slice_bitcast_fusion.16), channel_id=1, source_target_pairs={{0,32},{32,0},{64,96},{96,64},{1,33},{33,1},{65,97},{97,65},{2,34}... | collective-permute-start | bytes 1572872 | tf_op jit(solution)/shard_map/ppermute | solution.py:44
  196.0 10.8 %collective-permute-start.3 = (bf16[2,32,2048]{2,1,0:T(8,128)(2,1)S(1)}, bf16[2,32,2048]{2,1,0:T(8,128)(2,1)S(1)}, u32[]{:S(2)}, u32[]{:S(2)}) collective-permute-start(bf16[2,32,2048]{2,1,0:T(8,128)(2,1)S(1)} %slice_bitcast_fusion.26), channel_id=1, source_target_pairs={{0,64},{32,96},{64,0},{96,32},{1,65},{33,97},{65,1},{97,33},{2,66}... | collective-permute-start | bytes 786440 | tf_op jit(solution)/shard_map/ppermute | solution.py:44
  198.7 11.1 %collective-permute-start.7 = (bf16[2,32,2048]{2,1,0:T(8,128)(2,1)S(1)}, bf16[2,32,2048]{2,1,0:T(8,128)(2,1)S(1)}, u32[]{:S(2)}, u32[]{:S(2)}) collective-permute-start(bf16[2,32,2048]{2,1,0:T(8,128)(2,1)S(1)} %slice_bitcast_fusion.24), channel_id=1, source_target_pairs={{0,64},{32,96},{64,0},{96,32},{1,65},{33,97},{65,1},{97,33},{2,66}... | collective-permute-start | bytes 786440 | tf_op jit(solution)/shard_map/ppermute | solution.py:44
